TPU v7x, 256 devices: a whole 4x4x8 slice. The times are simulated.
256 devices in a mesh: ep: 32 (over z, x), tp: 8 (over y, core).
Axes of the slice: x: 4, y: 4, z: 8, core: 2. Of those that a mesh axis runs over, the one named last changes fastest.
Arguments:
- tokens: bfloat16 [4096, 7168], P('ep', 'tp'), may hold values from -6 to 6
- cotangent: bfloat16 [4096, 7168], P('ep', 'tp'), may hold values from -6 to 6
- expert_ids: int32 [4096, 8], P('ep'), may hold values from 0 to 31, all different within a row; in each aligned block of 128 rows (0 to 127, 128 to 255, ...) at most 36 rows name the same one
- gate_values: float32 [4096, 8], P('ep'), may hold values from 0.02 to 0.5
- w_gate: bfloat16 [32, 7168, 1024], P('ep', 'tp'), may hold values from -0.0625 to 0.0625
- w_up: bfloat16 [32, 7168, 1024], P('ep', 'tp'), may hold values from -0.0625 to 0.0625
- w_down: bfloat16 [32, 1024, 7168], P('ep', None, 'tp'), may hold values from -0.1875 to 0.1875
Outputs:
- mixed: bfloat16 [4096, 7168], P('ep', 'tp')
- d_tokens: bfloat16 [4096, 7168], P('ep', 'tp')
- d_gates: float32 [4096, 8], P('ep')
Inputs may be any that keep to these rules, and one draw needn't show every extreme that they name: `expert_ids`: each row names 8 different experts. Within each aligned block of 128 rows no expert is named by more than 36 rows, and in some block one expert is named by exactly 36 rows.
All inputs are finite; a program needn't handle non-finite values.
Results may differ from a plain program's by a relative error of at most 0.023.
Values may be sent and summed in bfloat16 or wider, within the bound.
No kernel may reach another device: no remote copies, remote signals or barrier semaphores. Data moves between devices by JAX's collectives and lax.ppermute only.
A program may use at most 64 MiB of HBM per device.

v0:
```python
import jax
import jax.numpy as jnp
from jax import lax
from jax.sharding import PartitionSpec as P

CAP = 36
SLOTS = CAP


def slot_tables(expert_ids, experts):
    count, topk = expert_ids.shape
    onehot = (expert_ids[:, :, None] == jnp.arange(experts, dtype=jnp.int32)[None, None, :]).astype(
        jnp.float32
    )
    present = jnp.sum(onehot, axis=1)
    earlier = (jnp.arange(count)[:, None] > jnp.arange(count)[None, :]).astype(jnp.float32)
    before = jnp.dot(earlier, present, precision=lax.Precision.HIGHEST).astype(jnp.int32)
    places = jnp.sum(before[:, None, :] * onehot.astype(jnp.int32), axis=2)
    slot = expert_ids * SLOTS + places
    total = experts * SLOTS
    picks = slot.T[:, :, None] == jnp.arange(total, dtype=jnp.int32)[None, None, :]
    dispatch = jnp.any(picks, axis=0).T.astype(jnp.bfloat16)
    return (picks, dispatch)


def local(tokens, cotangent, expert_ids, gate_values, w_gate, w_up, w_down):
    groups = lax.axis_size("ep")
    holders = w_gate.shape[0]
    experts = groups * holders
    units = w_gate.shape[2]
    picks, dispatch = slot_tables(expert_ids, experts)
    send_tokens = jnp.dot(dispatch, tokens, preferred_element_type=jnp.float32).astype(jnp.bfloat16)
    cot_rows = jnp.dot(dispatch, cotangent, preferred_element_type=jnp.float32)
    slot_gate = jnp.sum(jnp.where(picks, gate_values.T[:, :, None], 0.0), axis=(0, 1))
    send_scaled = (slot_gate[:, None] * cot_rows).astype(jnp.bfloat16)

    arrived = lax.all_to_all(send_tokens, "ep", 0, 0, tiled=True)
    arrived_grad = lax.all_to_all(send_scaled, "ep", 0, 0, tiled=True)

    wg = w_gate[0]
    wu = w_up[0]
    wd = w_down[0]
    joined_part = jnp.concatenate(
        [
            jnp.dot(arrived, wg, preferred_element_type=jnp.float32),
            jnp.dot(arrived, wu, preferred_element_type=jnp.float32),
        ],
        axis=1,
    ).astype(jnp.bfloat16)
    joined = lax.psum_scatter(joined_part, "tp", scatter_dimension=0, tiled=True).astype(jnp.float32)
    gate_in = joined[:, :units]
    up_in = joined[:, units:]
    sigma = jax.nn.sigmoid(gate_in)
    hidden = (gate_in * sigma * up_in).astype(jnp.bfloat16)
    outputs = jnp.dot(
        lax.all_gather(hidden, "tp", axis=0, tiled=True), wd, preferred_element_type=jnp.float32
    ).astype(jnp.bfloat16)
    returned = lax.all_to_all(outputs, "ep", 0, 0, tiled=True)

    d_hidden_part = lax.dot_general(
        arrived_grad, wd, (((1,), (1,)), ((), ())), preferred_element_type=jnp.float32
    ).astype(jnp.bfloat16)
    d_hidden = lax.psum_scatter(d_hidden_part, "tp", scatter_dimension=0, tiled=True).astype(
        jnp.float32
    )
    d_gate_in = (d_hidden * up_in * sigma * (1.0 + gate_in * (1.0 - sigma))).astype(jnp.bfloat16)
    d_up_in = (d_hidden * gate_in * sigma).astype(jnp.bfloat16)
    piece = lax.all_gather(jnp.concatenate([d_gate_in, d_up_in], axis=1), "tp", axis=0, tiled=True)
    contract = (((1,), (1,)), ((), ()))
    slot_grads = (
        lax.dot_general(piece[:, :units], wg, contract, preferred_element_type=jnp.float32)
        + lax.dot_general(piece[:, units:], wu, contract, preferred_element_type=jnp.float32)
    ).astype(jnp.bfloat16)
    returned_grad = lax.all_to_all(slot_grads, "ep", 0, 0, tiled=True)

    gather = picks.astype(jnp.bfloat16)
    out_slots = jnp.einsum("kts,sd->ktd", gather, returned, preferred_element_type=jnp.float32)
    mixed = jnp.sum(gate_values.T[:, :, None] * out_slots, axis=0).astype(jnp.bfloat16)
    partial_scores = jnp.sum(cotangent[None, :, :].astype(jnp.float32) * out_slots, axis=2).T
    d_gates = lax.psum(partial_scores, "tp")
    d_tokens = jnp.einsum(
        "ts,sd->td", jnp.sum(gather, axis=0), returned_grad, preferred_element_type=jnp.float32
    ).astype(jnp.bfloat16)
    return (mixed, d_tokens, d_gates)


def solution(mesh):
    in_specs = (
        P("ep", "tp"),
        P("ep", "tp"),
        P("ep", None),
        P("ep", None),
        P("ep", "tp", None),
        P("ep", "tp", None),
        P("ep", None, "tp"),
    )
    out_specs = (P("ep", "tp"), P("ep", "tp"), P("ep", None))
    return jax.shard_map(local, mesh=mesh, in_specs=in_specs, out_specs=out_specs, check_vma=False)
```

profile of v0, /device:TPU:24, one launch (start us, length us, event | category | flops | bytes accessed | tf_op | source)
XLA Modules:
  0.0 392.2 jit_solution(4935182646532571492)
XLA Ops:
  7.2 0.0 copy-start
  7.2 0.0 reduce-scatter.7.cloned.1.call-start
  7.2 0.8 convert_reduce_fusion
  8.1 0.2 convolution_convert_fusion.6
  8.2 0.8 fusion.22
  9.0 0.7 add_bitcast_fusion
  9.7 0.7 fusion.2
  10.4 3.0 convolution_convert_fusion.4
  13.4 3.9 %all_to_all.32 = bf16[32,36,896]{2,1,0:T(8,128)(2,1)} reshape(bf16[1152,896]{1,0:T(8,128)(2,1)} %convolution_convert_fusion.4) | data formatting | bytes 4128768 | tf_op jit(solution)/shard_map/all_to_all | solution.py:37
  17.3 68.0 %all_to_all.48 = bf16[32,36,896]{2,1,0:T(8,128)(2,1)} all-to-all(bf16[32,36,896]{2,1,0:T(8,128)(2,1)} %all_to_all.32), channel_id=1, replica_groups=mesh['ep'=32,'tp'=8] {'ep'}, dimensions={0} | all-to-all | bytes 4128768 | tf_op jit(solution)/shard_map/all_to_all | solution.py:37
  85.3 3.9 %all_to_all.34 = bf16[1152,896]{1,0:T(8,128)(2,1)} reshape(bf16[32,36,896]{2,1,0:T(8,128)(2,1)} %all_to_all.48) | data formatting | bytes 4128768 | tf_op jit(solution)/shard_map/all_to_all | solution.py:37
  89.3 0.0 copy-start.2
  89.3 0.0 copy-start.6
  89.3 5.1 %convolution_convert_fusion.1 = bf16[1152,1024]{0,1:T(8,128)(2,1)S(1)} fusion(bf16[1152,896]{1,0:T(8,128)(2,1)} %all_to_all.34, bf16[1,896,1024]{2,1,0:T(8,128)(2,1)} %param.12), kind=kOutput, calls=%fused_computation.9 | convolution fusion | flops 2115108864 | bytes 6258688 | tf_op jit(solution)/shard_map/dot_general | solution.py:46
  94.4 0.0 copy-done.2
  94.4 0.0 copy-done.6
  94.4 3.1 convolution_convert_fusion.2
  97.6 2.5 pad_maximum_fusion
  100.1 6.7 %copy.27 = bf16[1152,2048]{1,0:T(8,128)(2,1)} copy(bf16[1152,2048]{0,1:T(8,128)(2,1)} %pad_maximum_fusion) | data formatting | bytes 9437184
  106.8 0.0 copy-start.4
  106.8 0.0 copy-start.3
  106.8 0.0 reduce-scatter.7.cloned.1.call-update
  106.8 0.0 reduce-scatter.9.cloned.1.call-start
  106.9 0.6 copy-done.4
  107.5 0.6 select_reduce_fusion
  108.1 0.0 copy-done.3
  108.1 2.2 fusion.4
  110.3 4.0 %all_to_all.38 = bf16[32,36,896]{2,1,0:T(8,128)(2,1)} reshape(bf16[1152,896]{1,0:T(8,128)(2,1)} %fusion.4) | data formatting | bytes 4128768 | tf_op jit(solution)/shard_map/all_to_all | solution.py:38
  114.3 60.4 %all_to_all.49 = bf16[32,36,896]{2,1,0:T(8,128)(2,1)} all-to-all(bf16[32,36,896]{2,1,0:T(8,128)(2,1)} %all_to_all.38), channel_id=1, replica_groups=mesh['ep'=32,'tp'=8] {'ep'}, dimensions={0} | all-to-all | bytes 4128768 | tf_op jit(solution)/shard_map/all_to_all | solution.py:38
  174.6 3.9 %all_to_all.40 = bf16[1152,896]{1,0:T(8,128)(2,1)} reshape(bf16[32,36,896]{2,1,0:T(8,128)(2,1)} %all_to_all.49) | data formatting | bytes 4128768 | tf_op jit(solution)/shard_map/all_to_all | solution.py:38
  178.6 0.0 copy-done
  178.6 5.6 %convolution_convert_fusion = bf16[1152,1024]{1,0:T(8,128)(2,1)} fusion(bf16[1152,896]{1,0:T(8,128)(2,1)} %all_to_all.40, bf16[1,1024,896]{2,1,0:T(8,128)(2,1)S(1)} %copy-done), kind=kOutput, calls=%fused_computation.8 | convolution fusion | flops 2115108864 | bytes 6258688 | tf_op jit(solution)/shard_map/dot_general | solution.py:60
  184.1 0.0 reduce-scatter.9.cloned.1.call-update
  184.2 0.0 all-gather.3.cloned.1.call-start
  184.2 0.0 reduce-scatter.7.cloned.1.call-done
  184.2 1.2 convert_element_type.61
  185.4 27.5 %reduce-scatter.9.cloned.1.call-done = bf16[144,1024]{1,0:T(8,128)(2,1)} async-done(((bf16[1152,1024]{1,0:T(8,128)(2,1)}), bf16[144,1024]{1,0:T(8,128)(2,1)}) %reduce-scatter.9.cloned.1.call-update) | async-done | bytes 294928 | tf_op jit(solution)/shard_map/reduce_scatter | solution.py:63
  212.9 2.1 fusion.18
  215.0 0.0 all-gather.3.cloned.1.call-update
  215.0 0.2 all-gather.5.cloned.1.call-start
  215.3 1.8 pad_maximum_fusion.1
  217.1 0.0 all-gather.5.cloned.1.call-update
  217.1 27.4 %all-gather.3.cloned.1.call-done = bf16[1152,1024]{1,0:T(8,128)(2,1)} async-done(((bf16[144,1024]{1,0:T(8,128)(2,1)}), bf16[1152,1024]{1,0:T(8,128)(2,1)}) %all-gather.3.cloned.1.call-update) | async-done | bytes 2359312 | tf_op jit(solution)/shard_map/all_gather | solution.py:56
  244.5 5.6 %convolution_convert_fusion.3 = bf16[1152,896]{1,0:T(8,128)(2,1)} fusion(bf16[1152,1024]{1,0:T(8,128)(2,1)} %all-gather.3.cloned.1.call-done, bf16[1,1024,896]{2,1,0:T(8,128)(2,1)S(1)} %copy-done), kind=kOutput, calls=%fused_computation.15 | convolution fusion | flops 2114961408 | bytes 6258688 | tf_op jit(solution)/shard_map/dot_general | solution.py:55
  250.0 4.0 %all_to_all.35 = bf16[32,36,896]{2,1,0:T(8,128)(2,1)} reshape(bf16[1152,896]{1,0:T(8,128)(2,1)} %convolution_convert_fusion.3) | data formatting | bytes 4128768 | tf_op jit(solution)/shard_map/all_to_all | solution.py:58
  254.0 0.0 copy-start.7
  254.0 10.1 %all-to-all-start.1 = ((bf16[32,36,896]{2,1,0:T(8,128)(2,1)}), bf16[32,36,896]{2,1,0:T(8,128)(2,1)}, u32[]{:S(2)}, u32[]{:S(2)}) async-start(bf16[32,36,896]{2,1,0:T(8,128)(2,1)} %all_to_all.35), calls=%async_computation.1 | async-start | bytes 4587520 | tf_op jit(solution)/shard_map/all_to_all | solution.py:58
  264.1 18.6 %all-gather.5.cloned.1.call-done = bf16[1152,2048]{1,0:T(8,128)(2,1)} async-done(((bf16[144,2048]{1,0:T(8,128)(2,1)}), bf16[1152,2048]{1,0:T(8,128)(2,1)}) %all-gather.5.cloned.1.call-update) | async-done | bytes 4718608 | tf_op jit(solution)/shard_map/all_gather | solution.py:68
  282.7 0.0 copy-done.7
  282.7 4.5 %fusion.7 = f32[1152,896]{1,0:T(8,128)S(1)} fusion(bf16[1152,2048]{1,0:T(8,128)(2,1)} %all-gather.5.cloned.1.call-done, bf16[1,896,1024]{2,1,0:T(8,128)(2,1)S(1)} %copy-done.7), kind=kOutput, calls=%fused_computation.19 | convolution fusion | flops 2113929216 | bytes 8323072 | tf_op jit(solution)/shard_map/dot_general | solution.py:71
  287.2 0.0 copy-done.5
  287.2 0.0 copy-done.8
  287.2 3.9 fusion.3
  291.1 3.9 %all_to_all.41 = bf16[32,36,896]{2,1,0:T(8,128)(2,1)} reshape(bf16[1152,896]{1,0:T(8,128)(2,1)} %fusion.3) | data formatting | bytes 4128768 | tf_op jit(solution)/shard_map/all_to_all | solution.py:74
  295.0 23.8 %all-to-all-done.1 = bf16[32,36,896]{2,1,0:T(8,128)(2,1)} async-done(((bf16[32,36,896]{2,1,0:T(8,128)(2,1)}), bf16[32,36,896]{2,1,0:T(8,128)(2,1)}, u32[]{:S(2)}, u32[]{:S(2)}) %all-to-all-start.1) | async-done | bytes 2064416 | tf_op jit(solution)/shard_map/all_to_all | solution.py:58
  318.8 5.6 %all-to-all-start.3 = ((bf16[32,36,896]{2,1,0:T(8,128)(2,1)}), bf16[32,36,896]{2,1,0:T(8,128)(2,1)}, u32[]{:S(2)}, u32[]{:S(2)}) async-start(bf16[32,36,896]{2,1,0:T(8,128)(2,1)} %all_to_all.41), calls=%async_computation.3 | async-start | bytes 4587520 | tf_op jit(solution)/shard_map/all_to_all | solution.py:74
  324.4 0.6 fusion.5
  325.1 4.0 %reshape.21 = bf16[1152,896,1]{1,0,2:T(8,128)(2,1)} reshape(bf16[32,36,896]{2,1,0:T(8,128)(2,1)} %all-to-all-done.1) | data formatting | bytes 4128768 | tf_op jit(solution)/shard_map/all_to_all | solution.py:58
  329.1 5.4 %multiply_reduce_fusion = (f32[8,128]{1,0:T(8,128)S(1)}, bf16[128,896]{1,0:T(8,128)(2,1)}) fusion(f32[128,896]{1,0:T(8,128)S(1)} %convert_element_type.73, f32[8,128]{1,0:T(8,128)S(1)} %bitcast.35, bf16[1152,896,1]{1,0,2:T(8,128)(2,1)} %reshape.21, s32[8,128]{1,0:T(8,128)S(1)} %add_bitcast_fusion), kind=kOutput, calls=%fused_computation.11 | convolution fusion | flops 2118663168 | bytes 2764800 | tf_op jit(solution)/shard_map/kts,sd->ktd/dot_general | solution.py:77
  334.5 11.7 %psum.7 = f32[128,8]{0,1:T(8,128)} all-reduce(f32[128,8]{0,1:T(8,128)S(1)} %bitcast.33), channel_id=1, replica_groups=mesh['ep'=32,'tp'=8] {'tp'}, use_global_device_ids=true, to_apply=%region_9.10 | all-reduce | flops 1024 | bytes 8192 | tf_op jit(solution)/shard_map/psum | solution.py:80
  346.2 32.6 %all-to-all-done.3 = bf16[32,36,896]{2,1,0:T(8,128)(2,1)} async-done(((bf16[32,36,896]{2,1,0:T(8,128)(2,1)}), bf16[32,36,896]{2,1,0:T(8,128)(2,1)}, u32[]{:S(2)}, u32[]{:S(2)}) %all-to-all-start.3) | async-done | bytes 2064416 | tf_op jit(solution)/shard_map/all_to_all | solution.py:74
  378.8 4.1 %all_to_all.43 = bf16[1152,896]{1,0:T(8,128)(2,1)} reshape(bf16[32,36,896]{2,1,0:T(8,128)(2,1)} %all-to-all-done.3) | data formatting | bytes 4128768 | tf_op jit(solution)/shard_map/all_to_all | solution.py:74
  382.9 2.8 convolution_convert_fusion.5
  385.7 0.0 copy-done.1
  (4 shorter events, 0.0 us)
Async XLA Ops:
  7.2 171.4 %copy-start = (bf16[1,1024,896]{2,1,0:T(8,128)(2,1)S(1)}, bf16[1,1024,896]{2,1,0:T(8,128)(2,1)}, u32[]{:S(2)}) copy-start(bf16[1,1024,896]{2,1,0:T(8,128)(2,1)} %param.13) | copy-start | bytes 5505028
  7.2 177.1 %reduce-scatter.7.cloned.1.call-start = ((), (), s32[]{:S(2)}) async-start(), calls=%async_computation.8 | async-start | bytes 5308416 | tf_op jit(solution)/shard_map/reduce_scatter | solution.py:50
  89.3 5.1 %copy-start.2 = (bf16[1152,896]{1,0:T(8,128)(2,1)S(1)}, bf16[1152,896]{1,0:T(8,128)(2,1)}, u32[]{:S(2)}) copy-start(bf16[1152,896]{1,0:T(8,128)(2,1)} %all_to_all.34) | copy-start | bytes 6193156
  89.3 5.2 %copy-start.6 = (bf16[1,896,1024]{2,1,0:T(8,128)(2,1)S(1)}, bf16[1,896,1024]{2,1,0:T(8,128)(2,1)}, u32[]{:S(2)}) copy-start(bf16[1,896,1024]{2,1,0:T(8,128)(2,1)} %param.11) | copy-start | bytes 5505028
  106.8 0.7 copy-start.4
  106.8 1.3 copy-start.3
  106.8 106.1 %reduce-scatter.9.cloned.1.call-start = ((), (), s32[]{:S(2)}) async-start(), calls=%async_computation.9 | async-start | bytes 2654208 | tf_op jit(solution)/shard_map/reduce_scatter | solution.py:63
  184.2 60.3 %all-gather.3.cloned.1.call-start = ((), (), s32[]{:S(2)}) async-start(), calls=%async_computation.6 | async-start | bytes 2654208 | tf_op jit(solution)/shard_map/all_gather | solution.py:56
  215.0 67.6 %all-gather.5.cloned.1.call-start = ((), (), s32[]{:S(2)}) async-start(), calls=%async_computation.7 | async-start | bytes 5308416 | tf_op jit(solution)/shard_map/all_gather | solution.py:68
  254.0 28.6 %copy-start.7 = (bf16[1,896,1024]{2,1,0:T(8,128)(2,1)S(1)}, bf16[1,896,1024]{2,1,0:T(8,128)(2,1)}, u32[]{:S(2)}) copy-start(bf16[1,896,1024]{2,1,0:T(8,128)(2,1)} %param.11) | copy-start | bytes 5505028
  254.0 64.8 %all-to-all-start.1 = ((bf16[32,36,896]{2,1,0:T(8,128)(2,1)}), bf16[32,36,896]{2,1,0:T(8,128)(2,1)}, u32[]{:S(2)}, u32[]{:S(2)}) async-start(bf16[32,36,896]{2,1,0:T(8,128)(2,1)} %all_to_all.35), calls=%async_computation.1 | async-start | bytes 4587520 | tf_op jit(solution)/shard_map/all_to_all | solution.py:58
  282.7 4.5 %copy-start.5 = (bf16[1152,2048]{1,0:T(8,128)(2,1)S(1)}, bf16[1152,2048]{1,0:T(8,128)(2,1)}, u32[]{:S(2)}) copy-start(bf16[1152,2048]{1,0:T(8,128)(2,1)} %all-gather.5.cloned.1.call-done) | copy-start | bytes 14155780
  282.7 4.5 %copy-start.8 = (bf16[1,896,1024]{2,1,0:T(8,128)(2,1)S(1)}, bf16[1,896,1024]{2,1,0:T(8,128)(2,1)}, u32[]{:S(2)}) copy-start(bf16[1,896,1024]{2,1,0:T(8,128)(2,1)} %param.12) | copy-start | bytes 5505028
  318.8 60.0 %all-to-all-start.3 = ((bf16[32,36,896]{2,1,0:T(8,128)(2,1)}), bf16[32,36,896]{2,1,0:T(8,128)(2,1)}, u32[]{:S(2)}, u32[]{:S(2)}) async-start(bf16[32,36,896]{2,1,0:T(8,128)(2,1)} %all_to_all.41), calls=%async_computation.3 | async-start | bytes 4587520 | tf_op jit(solution)/shard_map/all_to_all | solution.py:74
  378.8 6.9 %copy-start.1 = (bf16[1,1024,896]{2,1,0:T(8,128)(2,1)S(1)}, bf16[1,1024,896]{2,1,0:T(8,128)(2,1)}, u32[]{:S(2)}) copy-start(bf16[1,1024,896]{2,1,0:T(8,128)(2,1)} %param.13) | copy-start | bytes 5505028
Sparse Core Ops, SparseCore 0:
  106.9 33.8 reduce-scatter.6
  184.3 28.5 reduce-scatter.8
  215.2 29.2 all-gather.2
  246.2 36.4 all-gather.4
where the time goes:
time: 395 us; the launch traced here: 392 us
  blocking collectives  140 us (35%)
  waiting for transfers between devices  130 us (33%)
  matrix products  41.3 us (10%)
  local copies, waits for them, and re-layouts  39.1 us (10%)
  starting transfers between devices  16 us (4%)
  between operations  13.9 us (4%)
  other arithmetic  12 us (3%)
    all_to_all x1, blocking collectives, local(): arrived = lax.all_to_all(send_tokens, 'ep', 0, 0, tiled=True)  68 us
    all_to_all x1, blocking collectives, local(): arrived_grad = lax.all_to_all(send_scaled, 'ep', 0, 0, tiled=True)  60.4 us
    all_to_all x1, waiting for transfers between devices, local(): returned_grad = lax.all_to_all(slot_grads, 'ep', 0, 0, tiled=True)  32.6 us
    reduce_scatter x1, waiting for transfers between devices, local(): lax.psum_scatter(d_hidden_part, 'tp', scatter_dimension=0, tiled=True)  27.5 us
    all_gather x1, waiting for transfers between devices, local(): lax.all_gather(hidden, 'tp', axis=0, tiled=True)  27.4 us
    all_to_all x1, waiting for transfers between devices, local(): returned = lax.all_to_all(outputs, 'ep', 0, 0, tiled=True)  23.8 us
    all_gather x1, waiting for transfers between devices, local(): lax.all_gather(jnp.concatenate([d_gate_in, d_up_in], axis=1), 'tp', axis=...  18.6 us
    psum x1, blocking collectives, local(): d_gates = lax.psum(partial_scores, 'tp')  11.7 us
  transfers between devices with their start and end apart: 6, of which 5 were waited for; matrix products, arithmetic and copies ran while one was open for 9% of the time, Pallas kernels for 0%

commit v1 on v0

v1 whole, which is shorter than its diff:
```python
import jax
import jax.numpy as jnp
from jax import lax
from jax.sharding import PartitionSpec as P

CAP = 36
SLOTS = CAP


def slot_tables(expert_ids, experts):
    count, topk = expert_ids.shape
    onehot = (expert_ids[:, :, None] == jnp.arange(experts, dtype=jnp.int32)[None, None, :]).astype(
        jnp.float32
    )
    present = jnp.sum(onehot, axis=1)
    earlier = (jnp.arange(count)[:, None] > jnp.arange(count)[None, :]).astype(jnp.float32)
    before = jnp.dot(earlier, present, precision=lax.Precision.HIGHEST).astype(jnp.int32)
    places = jnp.sum(before[:, None, :] * onehot.astype(jnp.int32), axis=2)
    picks = (expert_ids.T[:, :, None, None] == jnp.arange(experts, dtype=jnp.int32)[None, None, :, None]) & (
        places.T[:, :, None, None] == jnp.arange(SLOTS, dtype=jnp.int32)[None, None, None, :]
    )
    dispatch = jnp.any(picks, axis=0).astype(jnp.bfloat16)
    return (picks, dispatch)


def local(tokens, cotangent, expert_ids, gate_values, w_gate, w_up, w_down):
    groups = lax.axis_size("ep")
    holders = w_gate.shape[0]
    experts = groups * holders
    units = w_gate.shape[2]
    picks, dispatch = slot_tables(expert_ids, experts)
    send_tokens = jnp.einsum(
        "tgc,td->gcd", dispatch, tokens, preferred_element_type=jnp.float32
    ).astype(jnp.bfloat16)
    cot_rows = jnp.einsum("tgc,td->gcd", dispatch, cotangent, preferred_element_type=jnp.float32)
    slot_gate = jnp.sum(jnp.where(picks, gate_values.T[:, :, None, None], 0.0), axis=(0, 1))
    send_scaled = (slot_gate[:, :, None] * cot_rows).astype(jnp.bfloat16)

    arrived = lax.all_to_all(send_tokens, "ep", 0, 0, tiled=True)

    w_both = jnp.concatenate([w_gate[0], w_up[0]], axis=1)
    wd = w_down[0]
    joined_part = jnp.einsum(
        "gcd,df->gcf", arrived, w_both, preferred_element_type=jnp.float32
    ).astype(jnp.bfloat16)
    send_scaled, joined_part = lax.optimization_barrier((send_scaled, joined_part))
    arrived_grad = lax.all_to_all(send_scaled, "ep", 0, 0, tiled=True)
    joined = lax.psum_scatter(joined_part, "tp", scatter_dimension=0, tiled=True)
    arrived_grad, joined = lax.optimization_barrier((arrived_grad, joined))
    joined = joined.astype(jnp.float32)
    gate_in = joined[:, :, :units]
    up_in = joined[:, :, units:]
    sigma = jax.nn.sigmoid(gate_in)
    hidden = (gate_in * sigma * up_in).astype(jnp.bfloat16)
    hidden_all = lax.all_gather(hidden, "tp", axis=0, tiled=True)
    outputs = jnp.einsum("gcf,fd->gcd", hidden_all, wd, preferred_element_type=jnp.float32).astype(
        jnp.bfloat16
    )
    arrived_grad, outputs = lax.optimization_barrier((arrived_grad, outputs))
    returned = lax.all_to_all(outputs, "ep", 0, 0, tiled=True)
    d_hidden_part = jnp.einsum(
        "gcd,fd->gcf", arrived_grad, wd, preferred_element_type=jnp.float32
    ).astype(jnp.bfloat16)
    d_hidden = lax.psum_scatter(d_hidden_part, "tp", scatter_dimension=0, tiled=True).astype(
        jnp.float32
    )
    d_gate_in = (d_hidden * up_in * sigma * (1.0 + gate_in * (1.0 - sigma))).astype(jnp.bfloat16)
    d_up_in = (d_hidden * gate_in * sigma).astype(jnp.bfloat16)
    piece = lax.all_gather(jnp.concatenate([d_gate_in, d_up_in], axis=2), "tp", axis=0, tiled=True)
    slot_grads = jnp.einsum(
        "gcf,df->gcd", piece, w_both, preferred_element_type=jnp.float32
    ).astype(jnp.bfloat16)
    returned_grad = lax.all_to_all(slot_grads, "ep", 0, 0, tiled=True)

    gather = picks.astype(jnp.bfloat16)
    out_slots = jnp.einsum("ktgc,gcd->ktd", gather, returned, preferred_element_type=jnp.float32)
    mixed = jnp.sum(gate_values.T[:, :, None] * out_slots, axis=0).astype(jnp.bfloat16)
    partial_scores = jnp.sum(cotangent[None, :, :].astype(jnp.float32) * out_slots, axis=2).T
    d_gates = lax.psum(partial_scores, "tp")
    d_tokens = jnp.einsum(
        "tgc,gcd->td", dispatch, returned_grad, preferred_element_type=jnp.float32
    ).astype(jnp.bfloat16)
    return (mixed, d_tokens, d_gates)


def solution(mesh):
    in_specs = (
        P("ep", "tp"),
        P("ep", "tp"),
        P("ep", None),
        P("ep", None),
        P("ep", "tp", None),
        P("ep", "tp", None),
        P("ep", None, "tp"),
    )
    out_specs = (P("ep", "tp"), P("ep", "tp"), P("ep", None))
    return jax.shard_map(local, mesh=mesh, in_specs=in_specs, out_specs=out_specs, check_vma=False)
```

time: 395 us -> 361 us (0.914)
  blocking collectives: 140 us -> 73.6 us
  waiting for transfers between devices: 130 us -> 192 us
  local copies, waits for them, and re-layouts: 39.1 us -> 0.04 us
  starting transfers between devices: 16 us -> 29 us
    all_to_all x1 -> x0, blocking collectives: 68 us -> none  [local(): arrived = lax.all_to_all(send_tokens, 'ep', 0, 0, tiled=True)]
    all_to_all x0 -> x1, waiting for transfers between devices: none -> 51.2 us  [local(): arrived = lax.all_to_all(send_tokens, 'ep', 0, 0, tiled=True)]
    all_to_all x8 -> x0, local copies, waits for them, and re-layouts: 31.8 us -> none  [the longest x2 8.01 us: local(): returned_grad = lax.all_to_all(slot_grads, 'ep', 0, 0, tiled=True)]
    all_to_all x0 -> x1, starting transfers between devices: none -> 11.6 us  [local(): arrived = lax.all_to_all(send_tokens, 'ep', 0, 0, tiled=True)]
    reduce_scatter x1, waiting for transfers between devices: 27.5 us -> 35.6 us  [local(): lax.psum_scatter(d_hidden_part, 'tp', scatter_dimension=0, tiled=True)]
    all_to_all x1, waiting for transfers between devices: 23.8 us -> 15.8 us  [local(): returned = lax.all_to_all(outputs, 'ep', 0, 0, tiled=True)]
    unnamed x19 -> x16, local copies, waits for them, and re-layouts: 7.34 us -> 0.04 us
    all_gather x2, waiting for transfers between devices: 45.9 us -> 52.3 us  [the longest x1 29.3 us: local(): lax.all_gather(jnp.concatenate([d_gate_in, d_up_in], axis=2), 'tp', axis=...]
  transfers between devices with their start and end apart: 6 -> 7, of which waited for: 5 -> 6; matrix products, arithmetic and copies ran while one was open for 9% -> 5% of each run, Pallas kernels for 0% -> 0%
where the time goes in v1:
time: 361 us
  waiting for transfers between devices  192 us (53%)
  blocking collectives  73.6 us (20%)
  matrix products  44.1 us (12%)
  starting transfers between devices  29 us (8%)
  between operations  13.9 us (4%)
  other arithmetic  8.07 us (2%)
    all_to_all x1, blocking collectives, local(): arrived_grad = lax.all_to_all(send_scaled, 'ep', 0, 0, tiled=True)  61.8 us
    all_to_all x1, waiting for transfers between devices, local(): arrived = lax.all_to_all(send_tokens, 'ep', 0, 0, tiled=True)  51.2 us
    all_to_all x1, waiting for transfers between devices, local(): returned_grad = lax.all_to_all(slot_grads, 'ep', 0, 0, tiled=True)  37 us
    reduce_scatter x1, waiting for transfers between devices, local(): lax.psum_scatter(d_hidden_part, 'tp', scatter_dimension=0, tiled=True)  35.6 us
    all_gather x1, waiting for transfers between devices, local(): lax.all_gather(jnp.concatenate([d_gate_in, d_up_in], axis=2), 'tp', axis=...  29.3 us
    all_gather x1, waiting for transfers between devices, local(): hidden_all = lax.all_gather(hidden, 'tp', axis=0, tiled=True)  23 us
    all_to_all x1, waiting for transfers between devices, local(): returned = lax.all_to_all(outputs, 'ep', 0, 0, tiled=True)  15.8 us
    psum x1, blocking collectives, local(): d_gates = lax.psum(partial_scores, 'tp')  11.8 us
  transfers between devices with their start and end apart: 7, of which 6 were waited for; matrix products, arithmetic and copies ran while one was open for 5% of the time, Pallas kernels for 0%

profile of v1, /device:TPU:24, one launch (start us, length us, event | category | flops | bytes accessed | tf_op | source)
XLA Modules:
  0.0 360.5 jit_solution(14742736846958374770)
XLA Ops:
  7.2 0.0 copy-start
  7.2 0.8 convert_reduce_fusion
  8.0 0.2 convolution_convert_fusion.4
  8.2 0.8 fusion.21
  9.0 0.0 copy-start.3
  9.0 0.7 iota_compare_fusion.2
  9.7 0.0 copy-start.5
  9.7 0.5 and_reduce_fusion
  10.3 3.1 convolution_convert_fusion.3
  13.3 0.0 copy-start.7
  13.3 0.0 copy-start.2
  13.3 11.6 %all-to-all-start = ((bf16[32,36,896]{2,1,0:T(8,128)(2,1)}), bf16[32,36,896]{2,1,0:T(8,128)(2,1)}, u32[]{:S(2)}, u32[]{:S(2)}) async-start(bf16[32,36,896]{2,1,0:T(8,128)(2,1)} %convolution_convert_fusion.3), calls=%async_computation | async-start | bytes 4587520 | tf_op jit(solution)/shard_map/all_to_all | solution.py:39
  24.9 0.0 reduce-scatter.3.cloned.1.call-start
  24.9 0.0 copy-done.3
  25.0 0.0 copy-done.5
  25.0 0.0 copy-done.7
  25.0 0.9 fusion.2
  25.8 0.0 copy-done.2
  25.8 2.2 multiply_convert_fusion
  28.0 51.2 %all-to-all-done = bf16[32,36,896]{2,1,0:T(8,128)(2,1)} async-done(((bf16[32,36,896]{2,1,0:T(8,128)(2,1)}), bf16[32,36,896]{2,1,0:T(8,128)(2,1)}, u32[]{:S(2)}, u32[]{:S(2)}) %all-to-all-start) | async-done | bytes 2064416 | tf_op jit(solution)/shard_map/all_to_all | solution.py:39
  79.2 9.7 %convolution_convert_fusion = bf16[32,36,2048]{2,1,0:T(8,128)(2,1)} fusion(bf16[32,36,896]{2,1,0:T(8,128)(2,1)} %all-to-all-done, bf16[896,1024]{1,0:T(8,128)(2,1)} %bitcast.55, bf16[896,1024]{1,0:T(8,128)(2,1)} %bitcast.57), kind=kOutput, calls=%fused_computation.6 | convolution fusion | flops 4237557760 | bytes 10452992 | tf_op jit(solution)/shard_map/gcd,df->gcf/dot_general | solution.py:43
  88.9 0.0 reduce-scatter.3.cloned.1.call-update
  89.0 0.0 all-gather.3.cloned.1.call-start
  89.0 61.8 %all_to_all.20 = bf16[32,36,896]{2,1,0:T(8,128)(2,1)} all-to-all(bf16[32,36,896]{2,1,0:T(8,128)(2,1)} %multiply_convert_fusion), channel_id=1, replica_groups=mesh['ep'=32,'tp'=8] {'ep'}, dimensions={0} | all-to-all | bytes 4128768 | tf_op jit(solution)/shard_map/all_to_all | solution.py:47
  150.8 0.0 reduce-scatter.3.cloned.1.call-done
  150.8 1.2 convert_element_type.61
  152.0 0.9 multiply_convert_fusion.1
  153.0 0.0 all-gather.3.cloned.1.call-update
  153.0 0.0 reduce-scatter.5.cloned.1.call-start
  153.0 23.0 %all-gather.3.cloned.1.call-done = bf16[32,36,1024]{2,1,0:T(8,128)(2,1)} async-done(((bf16[4,36,1024]{2,1,0:T(8,128)(2,1)}), bf16[32,36,1024]{2,1,0:T(8,128)(2,1)}) %all-gather.3.cloned.1.call-update) | async-done | bytes 2359312 | tf_op jit(solution)/shard_map/all_gather | solution.py:55
  176.0 0.0 copy-done
  176.0 0.0 copy-start.1
  176.0 6.2 %convolution_convert_fusion.2 = bf16[32,36,896]{2,1,0:T(8,128)(2,1)} fusion(bf16[32,36,1024]{2,1,0:T(8,128)(2,1)} %all-gather.3.cloned.1.call-done, bf16[1,1024,896]{2,1,0:T(8,128)(2,1)S(1)} %copy-done), kind=kOutput, calls=%fused_computation.18 | convolution fusion | flops 2114961408 | bytes 6258688 | tf_op jit(solution)/shard_map/gcf,fd->gcd/dot_general | solution.py:56
  182.2 0.0 copy-done.1
  182.2 4.3 %convolution_convert_fusion.1 = bf16[32,36,1024]{2,1,0:T(8,128)(2,1)} fusion(bf16[32,36,896]{2,1,0:T(8,128)(2,1)S(1)} %copy-done.1, bf16[1,1024,896]{2,1,0:T(8,128)(2,1)S(1)} %copy-done), kind=kOutput, calls=%fused_computation.16 | convolution fusion | flops 2115108864 | bytes 6258688 | tf_op jit(solution)/shard_map/gcd,fd->gcf/dot_general | solution.py:61
  186.5 0.0 reduce-scatter.5.cloned.1.call-update
  186.6 0.0 all-gather.5.cloned.1.call-start
  186.6 35.6 %reduce-scatter.5.cloned.1.call-done = bf16[4,36,1024]{2,1,0:T(8,128)(2,1)} async-done(((bf16[32,36,1024]{2,1,0:T(8,128)(2,1)}), bf16[4,36,1024]{2,1,0:T(8,128)(2,1)}) %reduce-scatter.5.cloned.1.call-update) | async-done | bytes 294928 | tf_op jit(solution)/shard_map/reduce_scatter | solution.py:64
  222.3 1.3 fusion.15
  223.5 0.9 pad_maximum_fusion
  224.4 0.0 all-gather.5.cloned.1.call-update
  224.5 10.2 %all-to-all-start.2 = ((bf16[32,36,896]{2,1,0:T(8,128)(2,1)}), bf16[32,36,896]{2,1,0:T(8,128)(2,1)}, u32[]{:S(2)}, u32[]{:S(2)}) async-start(bf16[32,36,896]{2,1,0:T(8,128)(2,1)} %convolution_convert_fusion.2), calls=%async_computation.3 | async-start | bytes 4587520 | tf_op jit(solution)/shard_map/all_to_all | solution.py:60
  234.6 29.3 %all-gather.5.cloned.1.call-done = bf16[32,36,2048]{2,1,0:T(8,128)(2,1)} async-done(((bf16[4,36,2048]{2,1,0:T(8,128)(2,1)}), bf16[32,36,2048]{2,1,0:T(8,128)(2,1)}) %all-gather.5.cloned.1.call-update) | async-done | bytes 4718608 | tf_op jit(solution)/shard_map/all_gather | solution.py:69
  263.9 9.7 %fusion.9 = bf16[32,36,896]{2,1,0:T(8,128)(2,1)} fusion(bf16[32,36,2048]{2,1,0:T(8,128)(2,1)} %all-gather.5.cloned.1.call-done, bf16[896,1024]{1,0:T(8,128)(2,1)} %bitcast.56, bf16[896,1024]{1,0:T(8,128)(2,1)} %bitcast.58), kind=kOutput, calls=%fused_computation.17 | convolution fusion | flops 4236230656 | bytes 10452992 | tf_op jit(solution)/shard_map/gcf,df->gcd/dot_general | solution.py:70
  273.7 0.0 copy-start.4
  273.7 0.0 copy-start.6
  273.7 15.8 %all-to-all-done.2 = bf16[32,36,896]{2,1,0:T(8,128)(2,1)} async-done(((bf16[32,36,896]{2,1,0:T(8,128)(2,1)}), bf16[32,36,896]{2,1,0:T(8,128)(2,1)}, u32[]{:S(2)}, u32[]{:S(2)}) %all-to-all-start.2) | async-done | bytes 2064416 | tf_op jit(solution)/shard_map/all_to_all | solution.py:60
  289.4 7.1 %all-to-all-start.3 = ((bf16[32,36,896]{2,1,0:T(8,128)(2,1)}), bf16[32,36,896]{2,1,0:T(8,128)(2,1)}, u32[]{:S(2)}, u32[]{:S(2)}) async-start(bf16[32,36,896]{2,1,0:T(8,128)(2,1)} %fusion.9), calls=%async_computation.5 | async-start | bytes 4587520 | tf_op jit(solution)/shard_map/all_to_all | solution.py:73
  296.6 0.0 copy-done.4
  296.6 0.0 copy-done.6
  296.6 5.8 %fusion.4 = (f32[8,128]{1,0:T(8,128)S(1)}, bf16[128,896]{1,0:T(8,128)(2,1)}) fusion(f32[128,896]{1,0:T(8,128)S(1)} %convert_element_type.71, f32[8,128]{1,0:T(8,128)S(1)} %bitcast.53, bf16[32,36,896]{2,1,0:T(8,128)(2,1)} %all-to-all-done.2, pred[8,128,36]{1,2,0:T(8,128)(4,1)S(1)} %copy-done.4, pred[8,128,32]{1,2,0:T(8,128)(4,1)S(1)} %copy-done.6), kind=kOutput, calls=%fused_computation.11 | convolution fusion | flops 2118663168 | bytes 2830336 | tf_op jit(solution)/shard_map/ktgc,gcd->ktd/dot_general | solution.py:76
  302.4 11.8 %psum.7 = f32[128,8]{0,1:T(8,128)} all-reduce(f32[128,8]{0,1:T(8,128)S(1)} %bitcast.54), channel_id=1, replica_groups=mesh['ep'=32,'tp'=8] {'tp'}, use_global_device_ids=true, to_apply=%region_8.9 | all-reduce | flops 1024 | bytes 8192 | tf_op jit(solution)/shard_map/psum | solution.py:79
  314.1 37.0 %all-to-all-done.3 = bf16[32,36,896]{2,1,0:T(8,128)(2,1)} async-done(((bf16[32,36,896]{2,1,0:T(8,128)(2,1)}), bf16[32,36,896]{2,1,0:T(8,128)(2,1)}, u32[]{:S(2)}, u32[]{:S(2)}) %all-to-all-start.3) | async-done | bytes 2064416 | tf_op jit(solution)/shard_map/all_to_all | solution.py:73
  351.1 2.9 fusion.12
  (2 shorter events, 0.1 us)
Async XLA Ops:
  7.2 168.8 %copy-start = (bf16[1,1024,896]{2,1,0:T(8,128)(2,1)S(1)}, bf16[1,1024,896]{2,1,0:T(8,128)(2,1)}, u32[]{:S(2)}) copy-start(bf16[1,1024,896]{2,1,0:T(8,128)(2,1)} %param.13) | copy-start | bytes 5505028
  9.0 16.0 %copy-start.3 = (pred[8,128,36]{1,2,0:T(8,128)(4,1)}, pred[8,128,36]{1,2,0:T(8,128)(4,1)S(1)}, u32[]{:S(2)}) copy-start(pred[8,128,36]{1,2,0:T(8,128)(4,1)S(1)} %iota_compare_fusion) | copy-start | bytes 110596
  9.7 15.2 %copy-start.5 = (pred[8,128,32]{1,2,0:T(8,128)(4,1)}, pred[8,128,32]{1,2,0:T(8,128)(4,1)S(1)}, u32[]{:S(2)}) copy-start(pred[8,128,32]{1,2,0:T(8,128)(4,1)S(1)} %iota_compare_fusion.2) | copy-start | bytes 98308
  13.3 11.6 %copy-start.7 = (f32[128,8]{0,1:T(8,128)S(1)}, f32[128,8]{0,1:T(8,128)}, u32[]{:S(2)}) copy-start(f32[128,8]{0,1:T(8,128)} %param.10) | copy-start | bytes 12292
  13.3 12.5 %copy-start.2 = (bf16[128,896]{1,0:T(8,128)(2,1)S(1)}, bf16[128,896]{1,0:T(8,128)(2,1)}, u32[]{:S(2)}) copy-start(bf16[128,896]{1,0:T(8,128)(2,1)} %param.8) | copy-start | bytes 688132
  13.3 65.9 %all-to-all-start = ((bf16[32,36,896]{2,1,0:T(8,128)(2,1)}), bf16[32,36,896]{2,1,0:T(8,128)(2,1)}, u32[]{:S(2)}, u32[]{:S(2)}) async-start(bf16[32,36,896]{2,1,0:T(8,128)(2,1)} %convolution_convert_fusion.3), calls=%async_computation | async-start | bytes 4587520 | tf_op jit(solution)/shard_map/all_to_all | solution.py:39
  24.9 125.9 %reduce-scatter.3.cloned.1.call-start = ((), (), s32[]{:S(2)}) async-start(), calls=%async_computation.6 | async-start | bytes 5898240 | tf_op jit(solution)/shard_map/reduce_scatter | solution.py:48
  89.0 87.0 %all-gather.3.cloned.1.call-start = ((), (), s32[]{:S(2)}) async-start(), calls=%async_computation.7 | async-start | bytes 2949120 | tf_op jit(solution)/shard_map/all_gather | solution.py:55
  153.0 69.3 %reduce-scatter.5.cloned.1.call-start = ((), (), s32[]{:S(2)}) async-start(), calls=%async_computation.8 | async-start | bytes 2949120 | tf_op jit(solution)/shard_map/reduce_scatter | solution.py:64
  176.0 6.2 %copy-start.1 = (bf16[32,36,896]{2,1,0:T(8,128)(2,1)S(1)}, bf16[32,36,896]{2,1,0:T(8,128)(2,1)}, u32[]{:S(2)}) copy-start(bf16[32,36,896]{2,1,0:T(8,128)(2,1)} %all_to_all.20) | copy-start | bytes 6193156
  186.6 77.4 %all-gather.5.cloned.1.call-start = ((), (), s32[]{:S(2)}) async-start(), calls=%async_computation.9 | async-start | bytes 5898240 | tf_op jit(solution)/shard_map/all_gather | solution.py:69
  224.5 65.0 %all-to-all-start.2 = ((bf16[32,36,896]{2,1,0:T(8,128)(2,1)}), bf16[32,36,896]{2,1,0:T(8,128)(2,1)}, u32[]{:S(2)}, u32[]{:S(2)}) async-start(bf16[32,36,896]{2,1,0:T(8,128)(2,1)} %convolution_convert_fusion.2), calls=%async_computation.3 | async-start | bytes 4587520 | tf_op jit(solution)/shard_map/all_to_all | solution.py:60
  273.7 22.9 %copy-start.4 = (pred[8,128,36]{1,2,0:T(8,128)(4,1)S(1)}, pred[8,128,36]{1,2,0:T(8,128)(4,1)}, u32[]{:S(2)}) copy-start(pred[8,128,36]{1,2,0:T(8,128)(4,1)} %copy-done.3) | copy-start | bytes 110596
  273.7 22.9 %copy-start.6 = (pred[8,128,32]{1,2,0:T(8,128)(4,1)S(1)}, pred[8,128,32]{1,2,0:T(8,128)(4,1)}, u32[]{:S(2)}) copy-start(pred[8,128,32]{1,2,0:T(8,128)(4,1)} %copy-done.5) | copy-start | bytes 98308
  289.4 61.7 %all-to-all-start.3 = ((bf16[32,36,896]{2,1,0:T(8,128)(2,1)}), bf16[32,36,896]{2,1,0:T(8,128)(2,1)}, u32[]{:S(2)}, u32[]{:S(2)}) async-start(bf16[32,36,896]{2,1,0:T(8,128)(2,1)} %fusion.9), calls=%async_computation.5 | async-start | bytes 4587520 | tf_op jit(solution)/shard_map/all_to_all | solution.py:73
Sparse Core Ops, SparseCore 0:
  89.1 36.6 reduce-scatter.2
  153.1 22.8 all-gather.2
  186.7 35.5 reduce-scatter.4
  224.6 39.3 all-gather.4

commit v2 on v1

--- a/solution.py
+++ b/solution.py
@@ -2,13 +2,14 @@
 import jax.numpy as jnp
 from jax import lax
 from jax.sharding import PartitionSpec as P
+
 
 CAP = 36
 SLOTS = CAP
 
 
 def slot_tables(expert_ids, experts):
-    count, topk = expert_ids.shape
+    count, _ = expert_ids.shape
     onehot = (expert_ids[:, :, None] == jnp.arange(experts, dtype=jnp.int32)[None, None, :]).astype(
         jnp.float32
     )
@@ -23,7 +24,7 @@
     return (picks, dispatch)
 
 
-def local(tokens, cotangent, expert_ids, gate_values, w_gate, w_up, w_down):
+def body(tokens, cotangent, expert_ids, gate_values, w_gate, w_up, w_down):
     groups = lax.axis_size("ep")
     holders = w_gate.shape[0]
     experts = groups * holders
@@ -46,17 +47,16 @@
     send_scaled, joined_part = lax.optimization_barrier((send_scaled, joined_part))
     arrived_grad = lax.all_to_all(send_scaled, "ep", 0, 0, tiled=True)
     joined = lax.psum_scatter(joined_part, "tp", scatter_dimension=0, tiled=True)
-    arrived_grad, joined = lax.optimization_barrier((arrived_grad, joined))
     joined = joined.astype(jnp.float32)
     gate_in = joined[:, :, :units]
     up_in = joined[:, :, units:]
     sigma = jax.nn.sigmoid(gate_in)
     hidden = (gate_in * sigma * up_in).astype(jnp.bfloat16)
     hidden_all = lax.all_gather(hidden, "tp", axis=0, tiled=True)
+    arrived_grad, hidden_all = lax.optimization_barrier((arrived_grad, hidden_all))
     outputs = jnp.einsum("gcf,fd->gcd", hidden_all, wd, preferred_element_type=jnp.float32).astype(
         jnp.bfloat16
     )
-    arrived_grad, outputs = lax.optimization_barrier((arrived_grad, outputs))
     returned = lax.all_to_all(outputs, "ep", 0, 0, tiled=True)
     d_hidden_part = jnp.einsum(
         "gcd,fd->gcf", arrived_grad, wd, preferred_element_type=jnp.float32
@@ -94,4 +94,4 @@
         P("ep", None, "tp"),
     )
     out_specs = (P("ep", "tp"), P("ep", "tp"), P("ep", None))
-    return jax.shard_map(local, mesh=mesh, in_specs=in_specs, out_specs=out_specs, check_vma=False)
+    return jax.shard_map(body, mesh=mesh, in_specs=in_specs, out_specs=out_specs, check_vma=False)

time: 361 us -> 375 us (1.039)
  waiting for transfers between devices: 192 us -> 199 us
  blocking collectives: 73.6 us -> 78.2 us
    reduce_scatter x2, waiting for transfers between devices: 35.6 us -> 65.9 us  [the longest x1 35.8 us: body(): lax.psum_scatter(joined_part, 'tp', scatter_dimension=0, tiled=True)]
    all_gather x2, waiting for transfers between devices: 52.3 us -> 23.3 us  [the longest x1 23.3 us: body(): lax.all_gather(jnp.concatenate([d_gate_in, d_up_in], axis=2), 'tp', axis=...]
    all_to_all x3, waiting for transfers between devices: 104 us -> 110 us  [the longest x1 51.2 us: body(): arrived = lax.all_to_all(send_tokens, 'ep', 0, 0, tiled=True)]
    all_to_all x1, blocking collectives: 61.8 us -> 66.5 us  [body(): arrived_grad = lax.all_to_all(send_scaled, 'ep', 0, 0, tiled=True)]
  transfers between devices with their start and end apart: 7 -> 7, of which waited for: 6 -> 6; matrix products, arithmetic and copies ran while one was open for 5% -> 7% of each run, Pallas kernels for 0% -> 0%
where the time goes in v2:
time: 375 us; the launch traced here: 374 us
  waiting for transfers between devices  199 us (53%)
  blocking collectives  78.2 us (21%)
  matrix products  45.6 us (12%)
  starting transfers between devices  28.9 us (8%)
  between operations  13.9 us (4%)
  other arithmetic  8.12 us (2%)
    all_to_all x1, blocking collectives, body(): arrived_grad = lax.all_to_all(send_scaled, 'ep', 0, 0, tiled=True)  66.5 us
    all_to_all x1, waiting for transfers between devices, body(): arrived = lax.all_to_all(send_tokens, 'ep', 0, 0, tiled=True)  51.2 us
    all_to_all x1, waiting for transfers between devices, body(): returned_grad = lax.all_to_all(slot_grads, 'ep', 0, 0, tiled=True)  37 us
    reduce_scatter x1, waiting for transfers between devices, body(): lax.psum_scatter(joined_part, 'tp', scatter_dimension=0, tiled=True)  35.8 us
    reduce_scatter x1, waiting for transfers between devices, body(): lax.psum_scatter(d_hidden_part, 'tp', scatter_dimension=0, tiled=True)  30.1 us
    all_gather x1, waiting for transfers between devices, body(): lax.all_gather(jnp.concatenate([d_gate_in, d_up_in], axis=2), 'tp', axis=...  23.3 us
    all_to_all x1, waiting for transfers between devices, body(): returned = lax.all_to_all(outputs, 'ep', 0, 0, tiled=True)  21.7 us
    psum x1, blocking collectives, body(): d_gates = lax.psum(partial_scores, 'tp')  11.8 us
  transfers between devices with their start and end apart: 7, of which 6 were waited for; matrix products, arithmetic and copies ran while one was open for 7% of the time, Pallas kernels for 0%

profile of v2, /device:TPU:24, one launch (start us, length us, event | category | flops | bytes accessed | tf_op | source)
XLA Modules:
  0.0 373.9 jit_solution(228745265798498928)
XLA Ops:
  7.2 0.0 copy-start
  7.2 0.8 convert_reduce_fusion
  8.0 0.2 convolution_convert_fusion.4
  8.2 0.8 fusion.21
  9.0 0.0 copy-start.2
  9.0 0.7 iota_compare_fusion.2
  9.7 0.0 copy-start.4
  9.7 0.5 and_reduce_fusion
  10.3 3.1 convolution_convert_fusion.3
  13.3 0.0 copy-start.6
  13.3 0.0 copy-start.1
  13.3 11.6 %all-to-all-start = ((bf16[32,36,896]{2,1,0:T(8,128)(2,1)}), bf16[32,36,896]{2,1,0:T(8,128)(2,1)}, u32[]{:S(2)}, u32[]{:S(2)}) async-start(bf16[32,36,896]{2,1,0:T(8,128)(2,1)} %convolution_convert_fusion.3), calls=%async_computation | async-start | bytes 4587520 | tf_op jit(solution)/shard_map/all_to_all | solution.py:40
  24.9 0.0 reduce-scatter.3.cloned.1.call-start
  24.9 0.0 copy-done.2
  25.0 0.0 copy-done.4
  25.0 0.0 copy-done.6
  25.0 0.9 fusion.2
  25.8 0.0 copy-done.1
  25.8 2.2 multiply_convert_fusion
  28.0 51.2 %all-to-all-done = bf16[32,36,896]{2,1,0:T(8,128)(2,1)} async-done(((bf16[32,36,896]{2,1,0:T(8,128)(2,1)}), bf16[32,36,896]{2,1,0:T(8,128)(2,1)}, u32[]{:S(2)}, u32[]{:S(2)}) %all-to-all-start) | async-done | bytes 2064416 | tf_op jit(solution)/shard_map/all_to_all | solution.py:40
  79.2 9.7 %convolution_convert_fusion = bf16[32,36,2048]{2,1,0:T(8,128)(2,1)} fusion(bf16[32,36,896]{2,1,0:T(8,128)(2,1)} %all-to-all-done, bf16[896,1024]{1,0:T(8,128)(2,1)} %bitcast.55, bf16[896,1024]{1,0:T(8,128)(2,1)} %bitcast.57), kind=kOutput, calls=%fused_computation.6 | convolution fusion | flops 4237557760 | bytes 10452992 | tf_op jit(solution)/shard_map/gcd,df->gcf/dot_general | solution.py:44
  88.9 0.0 reduce-scatter.3.cloned.1.call-update
  89.0 0.0 all-gather.3.cloned.1.call-start
  89.0 35.8 %reduce-scatter.3.cloned.1.call-done = bf16[4,36,2048]{2,1,0:T(8,128)(2,1)} async-done(((bf16[32,36,2048]{2,1,0:T(8,128)(2,1)}), bf16[4,36,2048]{2,1,0:T(8,128)(2,1)}) %reduce-scatter.3.cloned.1.call-update) | async-done | bytes 589840 | tf_op jit(solution)/shard_map/reduce_scatter | solution.py:49
  124.8 1.2 convert_element_type.61
  126.0 0.9 multiply_convert_fusion.1
  126.9 0.0 all-gather.3.cloned.1.call-update
  127.0 0.0 reduce-scatter.5.cloned.1.call-start
  127.0 66.5 %all_to_all.20 = bf16[32,36,896]{2,1,0:T(8,128)(2,1)} all-to-all(bf16[32,36,896]{2,1,0:T(8,128)(2,1)} %multiply_convert_fusion), channel_id=1, replica_groups=mesh['ep'=32,'tp'=8] {'ep'}, dimensions={0} | all-to-all | bytes 4128768 | tf_op jit(solution)/shard_map/all_to_all | solution.py:48
  193.5 0.0 all-gather.3.cloned.1.call-done
  193.5 0.0 copy-done
  193.5 6.0 %convolution_convert_fusion.1 = bf16[32,36,1024]{2,1,0:T(8,128)(2,1)} fusion(bf16[32,36,896]{2,1,0:T(8,128)(2,1)} %all_to_all.20, bf16[1,1024,896]{2,1,0:T(8,128)(2,1)S(1)} %copy-done), kind=kOutput, calls=%fused_computation.16 | convolution fusion | flops 2115108864 | bytes 6258688 | tf_op jit(solution)/shard_map/gcd,fd->gcf/dot_general | solution.py:61
  199.5 0.0 reduce-scatter.5.cloned.1.call-update
  199.5 0.0 all-gather.5.cloned.1.call-start
  199.6 30.1 %reduce-scatter.5.cloned.1.call-done = bf16[4,36,1024]{2,1,0:T(8,128)(2,1)} async-done(((bf16[32,36,1024]{2,1,0:T(8,128)(2,1)}), bf16[4,36,1024]{2,1,0:T(8,128)(2,1)}) %reduce-scatter.5.cloned.1.call-update) | async-done | bytes 294928 | tf_op jit(solution)/shard_map/reduce_scatter | solution.py:64
  229.7 1.3 fusion.15
  231.0 0.9 pad_maximum_fusion
  231.9 0.0 all-gather.5.cloned.1.call-update
  232.0 6.1 %convolution_convert_fusion.2 = bf16[32,36,896]{2,1,0:T(8,128)(2,1)} fusion(bf16[32,36,1024]{2,1,0:T(8,128)(2,1)} %all-gather.3.cloned.1.call-done, bf16[1,1024,896]{2,1,0:T(8,128)(2,1)S(1)} %copy-done), kind=kOutput, calls=%fused_computation.18 | convolution fusion | flops 2114961408 | bytes 6258688 | tf_op jit(solution)/shard_map/gcf,fd->gcd/dot_general | solution.py:57
  238.0 10.1 %all-to-all-start.2 = ((bf16[32,36,896]{2,1,0:T(8,128)(2,1)}), bf16[32,36,896]{2,1,0:T(8,128)(2,1)}, u32[]{:S(2)}, u32[]{:S(2)}) async-start(bf16[32,36,896]{2,1,0:T(8,128)(2,1)} %convolution_convert_fusion.2), calls=%async_computation.3 | async-start | bytes 4587520 | tf_op jit(solution)/shard_map/all_to_all | solution.py:60
  248.1 23.3 %all-gather.5.cloned.1.call-done = bf16[32,36,2048]{2,1,0:T(8,128)(2,1)} async-done(((bf16[4,36,2048]{2,1,0:T(8,128)(2,1)}), bf16[32,36,2048]{2,1,0:T(8,128)(2,1)}) %all-gather.5.cloned.1.call-update) | async-done | bytes 4718608 | tf_op jit(solution)/shard_map/all_gather | solution.py:69
  271.4 9.7 %fusion.9 = bf16[32,36,896]{2,1,0:T(8,128)(2,1)} fusion(bf16[32,36,2048]{2,1,0:T(8,128)(2,1)} %all-gather.5.cloned.1.call-done, bf16[896,1024]{1,0:T(8,128)(2,1)} %bitcast.56, bf16[896,1024]{1,0:T(8,128)(2,1)} %bitcast.58), kind=kOutput, calls=%fused_computation.17 | convolution fusion | flops 4236230656 | bytes 10452992 | tf_op jit(solution)/shard_map/gcf,df->gcd/dot_general | solution.py:70
  281.1 0.0 copy-start.3
  281.1 0.0 copy-start.5
  281.1 21.7 %all-to-all-done.2 = bf16[32,36,896]{2,1,0:T(8,128)(2,1)} async-done(((bf16[32,36,896]{2,1,0:T(8,128)(2,1)}), bf16[32,36,896]{2,1,0:T(8,128)(2,1)}, u32[]{:S(2)}, u32[]{:S(2)}) %all-to-all-start.2) | async-done | bytes 2064416 | tf_op jit(solution)/shard_map/all_to_all | solution.py:60
  302.8 7.1 %all-to-all-start.3 = ((bf16[32,36,896]{2,1,0:T(8,128)(2,1)}), bf16[32,36,896]{2,1,0:T(8,128)(2,1)}, u32[]{:S(2)}, u32[]{:S(2)}) async-start(bf16[32,36,896]{2,1,0:T(8,128)(2,1)} %fusion.9), calls=%async_computation.5 | async-start | bytes 4587520 | tf_op jit(solution)/shard_map/all_to_all | solution.py:73
  310.0 0.0 copy-done.3
  310.0 0.0 copy-done.5
  310.0 5.8 %fusion.4 = (f32[8,128]{1,0:T(8,128)S(1)}, bf16[128,896]{1,0:T(8,128)(2,1)}) fusion(f32[128,896]{1,0:T(8,128)S(1)} %convert_element_type.71, f32[8,128]{1,0:T(8,128)S(1)} %bitcast.53, bf16[32,36,896]{2,1,0:T(8,128)(2,1)} %all-to-all-done.2, pred[8,128,36]{1,2,0:T(8,128)(4,1)S(1)} %copy-done.3, pred[8,128,32]{1,2,0:T(8,128)(4,1)S(1)} %copy-done.5), kind=kOutput, calls=%fused_computation.11 | convolution fusion | flops 2118663168 | bytes 2830336 | tf_op jit(solution)/shard_map/ktgc,gcd->ktd/dot_general | solution.py:76
  315.8 11.8 %psum.7 = f32[128,8]{0,1:T(8,128)} all-reduce(f32[128,8]{0,1:T(8,128)S(1)} %bitcast.54), channel_id=1, replica_groups=mesh['ep'=32,'tp'=8] {'tp'}, use_global_device_ids=true, to_apply=%region_8.9 | all-reduce | flops 1024 | bytes 8192 | tf_op jit(solution)/shard_map/psum | solution.py:79
  327.5 37.0 %all-to-all-done.3 = bf16[32,36,896]{2,1,0:T(8,128)(2,1)} async-done(((bf16[32,36,896]{2,1,0:T(8,128)(2,1)}), bf16[32,36,896]{2,1,0:T(8,128)(2,1)}, u32[]{:S(2)}, u32[]{:S(2)}) %all-to-all-start.3) | async-done | bytes 2064416 | tf_op jit(solution)/shard_map/all_to_all | solution.py:73
  364.5 2.9 fusion.12
  (2 shorter events, 0.1 us)
Async XLA Ops:
  7.2 186.3 %copy-start = (bf16[1,1024,896]{2,1,0:T(8,128)(2,1)S(1)}, bf16[1,1024,896]{2,1,0:T(8,128)(2,1)}, u32[]{:S(2)}) copy-start(bf16[1,1024,896]{2,1,0:T(8,128)(2,1)} %param.13) | copy-start | bytes 5505028
  9.0 16.0 %copy-start.2 = (pred[8,128,36]{1,2,0:T(8,128)(4,1)}, pred[8,128,36]{1,2,0:T(8,128)(4,1)S(1)}, u32[]{:S(2)}) copy-start(pred[8,128,36]{1,2,0:T(8,128)(4,1)S(1)} %iota_compare_fusion) | copy-start | bytes 110596
  9.7 15.2 %copy-start.4 = (pred[8,128,32]{1,2,0:T(8,128)(4,1)}, pred[8,128,32]{1,2,0:T(8,128)(4,1)S(1)}, u32[]{:S(2)}) copy-start(pred[8,128,32]{1,2,0:T(8,128)(4,1)S(1)} %iota_compare_fusion.2) | copy-start | bytes 98308
  13.3 11.6 %copy-start.6 = (f32[128,8]{0,1:T(8,128)S(1)}, f32[128,8]{0,1:T(8,128)}, u32[]{:S(2)}) copy-start(f32[128,8]{0,1:T(8,128)} %param.10) | copy-start | bytes 12292
  13.3 12.5 %copy-start.1 = (bf16[128,896]{1,0:T(8,128)(2,1)S(1)}, bf16[128,896]{1,0:T(8,128)(2,1)}, u32[]{:S(2)}) copy-start(bf16[128,896]{1,0:T(8,128)(2,1)} %param.8) | copy-start | bytes 688132
  13.3 65.9 %all-to-all-start = ((bf16[32,36,896]{2,1,0:T(8,128)(2,1)}), bf16[32,36,896]{2,1,0:T(8,128)(2,1)}, u32[]{:S(2)}, u32[]{:S(2)}) async-start(bf16[32,36,896]{2,1,0:T(8,128)(2,1)} %convolution_convert_fusion.3), calls=%async_computation | async-start | bytes 4587520 | tf_op jit(solution)/shard_map/all_to_all | solution.py:40
  24.9 99.9 %reduce-scatter.3.cloned.1.call-start = ((), (), s32[]{:S(2)}) async-start(), calls=%async_computation.6 | async-start | bytes 5898240 | tf_op jit(solution)/shard_map/reduce_scatter | solution.py:49
  89.0 104.5 %all-gather.3.cloned.1.call-start = ((), (), s32[]{:S(2)}) async-start(), calls=%async_computation.7 | async-start | bytes 2949120 | tf_op jit(solution)/shard_map/all_gather | solution.py:55
  127.0 102.8 %reduce-scatter.5.cloned.1.call-start = ((), (), s32[]{:S(2)}) async-start(), calls=%async_computation.8 | async-start | bytes 2949120 | tf_op jit(solution)/shard_map/reduce_scatter | solution.py:64
  199.5 71.9 %all-gather.5.cloned.1.call-start = ((), (), s32[]{:S(2)}) async-start(), calls=%async_computation.9 | async-start | bytes 5898240 | tf_op jit(solution)/shard_map/all_gather | solution.py:69
  238.0 64.8 %all-to-all-start.2 = ((bf16[32,36,896]{2,1,0:T(8,128)(2,1)}), bf16[32,36,896]{2,1,0:T(8,128)(2,1)}, u32[]{:S(2)}, u32[]{:S(2)}) async-start(bf16[32,36,896]{2,1,0:T(8,128)(2,1)} %convolution_convert_fusion.2), calls=%async_computation.3 | async-start | bytes 4587520 | tf_op jit(solution)/shard_map/all_to_all | solution.py:60
  281.1 28.9 %copy-start.3 = (pred[8,128,36]{1,2,0:T(8,128)(4,1)S(1)}, pred[8,128,36]{1,2,0:T(8,128)(4,1)}, u32[]{:S(2)}) copy-start(pred[8,128,36]{1,2,0:T(8,128)(4,1)} %copy-done.2) | copy-start | bytes 110596
  281.1 28.9 %copy-start.5 = (pred[8,128,32]{1,2,0:T(8,128)(4,1)S(1)}, pred[8,128,32]{1,2,0:T(8,128)(4,1)}, u32[]{:S(2)}) copy-start(pred[8,128,32]{1,2,0:T(8,128)(4,1)} %copy-done.4) | copy-start | bytes 98308
  302.8 61.7 %all-to-all-start.3 = ((bf16[32,36,896]{2,1,0:T(8,128)(2,1)}), bf16[32,36,896]{2,1,0:T(8,128)(2,1)}, u32[]{:S(2)}, u32[]{:S(2)}) async-start(bf16[32,36,896]{2,1,0:T(8,128)(2,1)} %fusion.9), calls=%async_computation.5 | async-start | bytes 4587520 | tf_op jit(solution)/shard_map/all_to_all | solution.py:73
Sparse Core Ops, SparseCore 0:
  89.1 35.6 reduce-scatter.2
  127.1 30.8 all-gather.2
  199.6 30.0 reduce-scatter.4
  232.1 39.2 all-gather.4

commit v3 on v2

--- a/solution.py
+++ b/solution.py
@@ -53,7 +53,6 @@
     sigma = jax.nn.sigmoid(gate_in)
     hidden = (gate_in * sigma * up_in).astype(jnp.bfloat16)
     hidden_all = lax.all_gather(hidden, "tp", axis=0, tiled=True)
-    arrived_grad, hidden_all = lax.optimization_barrier((arrived_grad, hidden_all))
     outputs = jnp.einsum("gcf,fd->gcd", hidden_all, wd, preferred_element_type=jnp.float32).astype(
         jnp.bfloat16
     )
@@ -64,6 +63,10 @@
     d_hidden = lax.psum_scatter(d_hidden_part, "tp", scatter_dimension=0, tiled=True).astype(
         jnp.float32
     )
+    d_hidden, joined = lax.optimization_barrier((d_hidden, joined))
+    gate_in = joined[:, :, :units]
+    up_in = joined[:, :, units:]
+    sigma = jax.nn.sigmoid(gate_in)
     d_gate_in = (d_hidden * up_in * sigma * (1.0 + gate_in * (1.0 - sigma))).astype(jnp.bfloat16)
     d_up_in = (d_hidden * gate_in * sigma).astype(jnp.bfloat16)
     piece = lax.all_gather(jnp.concatenate([d_gate_in, d_up_in], axis=2), "tp", axis=0, tiled=True)

time: 375 us -> 358 us (0.955)
  waiting for transfers between devices: 199 us -> 190 us
  blocking collectives: 78.2 us -> 73.3 us
    reduce_scatter x1, waiting for transfers between devices: 35.8 us -> 0.02 us  [body(): lax.psum_scatter(joined_part, 'tp', scatter_dimension=0, tiled=True)]
    all_gather x1, waiting for transfers between devices: 0.01 us -> 29.3 us  [body(): hidden_all = lax.all_gather(hidden, 'tp', axis=0, tiled=True)]
    all_to_all x1, blocking collectives: 66.5 us -> 61.7 us  [body(): arrived_grad = lax.all_to_all(send_scaled, 'ep', 0, 0, tiled=True)]
  transfers between devices with their start and end apart: 7 -> 7, of which waited for: 6 -> 6; matrix products, arithmetic and copies ran while one was open for 7% -> 9% of each run, Pallas kernels for 0% -> 0%
where the time goes in v3:
time: 358 us; the launch traced here: 356 us
  waiting for transfers between devices  190 us (53%)
  blocking collectives  73.3 us (20%)
  matrix products  44 us (12%)
  starting transfers between devices  27.4 us (8%)
  between operations  13.9 us (4%)
  other arithmetic  8.27 us (2%)
    all_to_all x1, blocking collectives, body(): arrived_grad = lax.all_to_all(send_scaled, 'ep', 0, 0, tiled=True)  61.7 us
    all_to_all x1, waiting for transfers between devices, body(): arrived = lax.all_to_all(send_tokens, 'ep', 0, 0, tiled=True)  51.2 us
    all_to_all x1, waiting for transfers between devices, body(): returned_grad = lax.all_to_all(slot_grads, 'ep', 0, 0, tiled=True)  37 us
    all_gather x1, waiting for transfers between devices, body(): hidden_all = lax.all_gather(hidden, 'tp', axis=0, tiled=True)  29.3 us
    reduce_scatter x1, waiting for transfers between devices, body(): lax.psum_scatter(d_hidden_part, 'tp', scatter_dimension=0, tiled=True)  27.2 us
    all_gather x1, waiting for transfers between devices, body(): lax.all_gather(jnp.concatenate([d_gate_in, d_up_in], axis=2), 'tp', axis=...  24 us
    all_to_all x1, waiting for transfers between devices, body(): returned = lax.all_to_all(outputs, 'ep', 0, 0, tiled=True)  20.8 us
    psum x1, blocking collectives, body(): d_gates = lax.psum(partial_scores, 'tp')  11.6 us
  transfers between devices with their start and end apart: 7, of which 6 were waited for; matrix products, arithmetic and copies ran while one was open for 9% of the time, Pallas kernels for 0%

profile of v3, /device:TPU:24, one launch (start us, length us, event | category | flops | bytes accessed | tf_op | source)
XLA Modules:
  0.0 356.4 jit_solution(10595943534566793842)
XLA Ops:
  7.2 0.0 copy-start
  7.2 0.8 convert_reduce_fusion
  8.0 0.2 convolution_convert_fusion.4
  8.2 0.8 fusion.17
  9.0 0.0 copy-start.2
  9.0 0.7 iota_compare_fusion.2
  9.7 0.0 copy-start.4
  9.7 0.5 and_reduce_fusion
  10.3 3.1 convolution_convert_fusion.3
  13.3 0.0 copy-start.6
  13.3 0.0 copy-start.1
  13.3 11.6 %all-to-all-start = ((bf16[32,36,896]{2,1,0:T(8,128)(2,1)}), bf16[32,36,896]{2,1,0:T(8,128)(2,1)}, u32[]{:S(2)}, u32[]{:S(2)}) async-start(bf16[32,36,896]{2,1,0:T(8,128)(2,1)} %convolution_convert_fusion.3), calls=%async_computation | async-start | bytes 4587520 | tf_op jit(solution)/shard_map/all_to_all | solution.py:40
  24.9 0.0 reduce-scatter.3.cloned.1.call-start
  24.9 0.0 copy-done.2
  25.0 0.0 copy-done.4
  25.0 0.0 copy-done.6
  25.0 0.9 fusion.2
  25.8 0.0 copy-done.1
  25.8 2.2 multiply_convert_fusion
  28.0 51.2 %all-to-all-done = bf16[32,36,896]{2,1,0:T(8,128)(2,1)} async-done(((bf16[32,36,896]{2,1,0:T(8,128)(2,1)}), bf16[32,36,896]{2,1,0:T(8,128)(2,1)}, u32[]{:S(2)}, u32[]{:S(2)}) %all-to-all-start) | async-done | bytes 2064416 | tf_op jit(solution)/shard_map/all_to_all | solution.py:40
  79.2 9.7 %convolution_convert_fusion = bf16[32,36,2048]{2,1,0:T(8,128)(2,1)} fusion(bf16[32,36,896]{2,1,0:T(8,128)(2,1)} %all-to-all-done, bf16[896,1024]{1,0:T(8,128)(2,1)} %bitcast.55, bf16[896,1024]{1,0:T(8,128)(2,1)} %bitcast.57), kind=kOutput, calls=%fused_computation.6 | convolution fusion | flops 4237557760 | bytes 10452992 | tf_op jit(solution)/shard_map/gcd,df->gcf/dot_general | solution.py:44
  88.9 0.0 reduce-scatter.3.cloned.1.call-update
  89.0 0.0 reduce-scatter.5.cloned.1.call-start
  89.0 61.7 %all_to_all.20 = bf16[32,36,896]{2,1,0:T(8,128)(2,1)S(1)} all-to-all(bf16[32,36,896]{2,1,0:T(8,128)(2,1)} %multiply_convert_fusion), channel_id=1, replica_groups=mesh['ep'=32,'tp'=8] {'ep'}, dimensions={0} | all-to-all | bytes 4128768 | tf_op jit(solution)/shard_map/all_to_all | solution.py:48
  150.7 0.0 copy-done
  150.7 4.3 %convolution_convert_fusion.1 = bf16[32,36,1024]{2,1,0:T(8,128)(2,1)} fusion(bf16[32,36,896]{2,1,0:T(8,128)(2,1)S(1)} %all_to_all.20, bf16[1,1024,896]{2,1,0:T(8,128)(2,1)S(1)} %copy-done), kind=kOutput, calls=%fused_computation.16 | convolution fusion | flops 2115108864 | bytes 6258688 | tf_op jit(solution)/shard_map/gcd,fd->gcf/dot_general | solution.py:60
  155.0 0.0 reduce-scatter.5.cloned.1.call-update
  155.1 0.0 all-gather.3.cloned.1.call-start
  155.1 0.0 reduce-scatter.3.cloned.1.call-done
  155.1 1.2 convert_element_type.61
  156.4 0.9 fusion.13
  157.3 0.0 all-gather.3.cloned.1.call-update
  157.3 0.0 all-gather.5.cloned.1.call-start
  157.4 27.2 %reduce-scatter.5.cloned.1.call-done = bf16[4,36,1024]{2,1,0:T(8,128)(2,1)} async-done(((bf16[32,36,1024]{2,1,0:T(8,128)(2,1)}), bf16[4,36,1024]{2,1,0:T(8,128)(2,1)}) %reduce-scatter.5.cloned.1.call-update) | async-done | bytes 294928 | tf_op jit(solution)/shard_map/reduce_scatter | solution.py:63
  184.5 1.0 convert_element_type.66
  185.6 0.4 multiply_convert_fusion.2
  186.0 0.9 pad_maximum_fusion
  186.9 0.0 all-gather.5.cloned.1.call-update
  186.9 29.3 %all-gather.3.cloned.1.call-done = bf16[32,36,1024]{2,1,0:T(8,128)(2,1)} async-done(((bf16[4,36,1024]{2,1,0:T(8,128)(2,1)}), bf16[32,36,1024]{2,1,0:T(8,128)(2,1)}) %all-gather.3.cloned.1.call-update) | async-done | bytes 2359312 | tf_op jit(solution)/shard_map/all_gather | solution.py:55
  216.3 6.1 %convolution_convert_fusion.2 = bf16[32,36,896]{2,1,0:T(8,128)(2,1)} fusion(bf16[32,36,1024]{2,1,0:T(8,128)(2,1)} %all-gather.3.cloned.1.call-done, bf16[1,1024,896]{2,1,0:T(8,128)(2,1)S(1)} %copy-done), kind=kOutput, calls=%fused_computation.18 | convolution fusion | flops 2114961408 | bytes 6258688 | tf_op jit(solution)/shard_map/gcf,fd->gcd/dot_general | solution.py:56
  222.4 10.1 %all-to-all-start.1 = ((bf16[32,36,896]{2,1,0:T(8,128)(2,1)}), bf16[32,36,896]{2,1,0:T(8,128)(2,1)}, u32[]{:S(2)}, u32[]{:S(2)}) async-start(bf16[32,36,896]{2,1,0:T(8,128)(2,1)} %convolution_convert_fusion.2), calls=%async_computation.2 | async-start | bytes 4587520 | tf_op jit(solution)/shard_map/all_to_all | solution.py:59
  232.5 24.0 %all-gather.5.cloned.1.call-done = bf16[32,36,2048]{2,1,0:T(8,128)(2,1)} async-done(((bf16[4,36,2048]{2,1,0:T(8,128)(2,1)}), bf16[32,36,2048]{2,1,0:T(8,128)(2,1)}) %all-gather.5.cloned.1.call-update) | async-done | bytes 4718608 | tf_op jit(solution)/shard_map/all_gather | solution.py:72
  256.5 9.7 %fusion.9 = bf16[32,36,896]{2,1,0:T(8,128)(2,1)} fusion(bf16[32,36,2048]{2,1,0:T(8,128)(2,1)} %all-gather.5.cloned.1.call-done, bf16[896,1024]{1,0:T(8,128)(2,1)} %bitcast.56, bf16[896,1024]{1,0:T(8,128)(2,1)} %bitcast.58), kind=kOutput, calls=%fused_computation.17 | convolution fusion | flops 4236230656 | bytes 10452992 | tf_op jit(solution)/shard_map/gcf,df->gcd/dot_general | solution.py:73
  266.2 0.0 copy-start.3
  266.2 0.0 copy-start.5
  266.2 20.8 %all-to-all-done.1 = bf16[32,36,896]{2,1,0:T(8,128)(2,1)} async-done(((bf16[32,36,896]{2,1,0:T(8,128)(2,1)}), bf16[32,36,896]{2,1,0:T(8,128)(2,1)}, u32[]{:S(2)}, u32[]{:S(2)}) %all-to-all-start.1) | async-done | bytes 2064416 | tf_op jit(solution)/shard_map/all_to_all | solution.py:59
  287.0 5.6 %all-to-all-start.3 = ((bf16[32,36,896]{2,1,0:T(8,128)(2,1)}), bf16[32,36,896]{2,1,0:T(8,128)(2,1)}, u32[]{:S(2)}, u32[]{:S(2)}) async-start(bf16[32,36,896]{2,1,0:T(8,128)(2,1)} %fusion.9), calls=%async_computation.5 | async-start | bytes 4587520 | tf_op jit(solution)/shard_map/all_to_all | solution.py:76
  292.6 0.0 copy-done.3
  292.6 0.0 copy-done.5
  292.6 5.8 %fusion.4 = (f32[8,128]{1,0:T(8,128)S(1)}, bf16[128,896]{1,0:T(8,128)(2,1)}) fusion(f32[128,896]{1,0:T(8,128)S(1)} %convert_element_type.71, f32[8,128]{1,0:T(8,128)S(1)} %bitcast.53, bf16[32,36,896]{2,1,0:T(8,128)(2,1)} %all-to-all-done.1, pred[8,128,36]{1,2,0:T(8,128)(4,1)S(1)} %copy-done.3, pred[8,128,32]{1,2,0:T(8,128)(4,1)S(1)} %copy-done.5), kind=kOutput, calls=%fused_computation.11 | convolution fusion | flops 2118663168 | bytes 2830336 | tf_op jit(solution)/shard_map/ktgc,gcd->ktd/dot_general | solution.py:79
  298.4 11.6 %psum.7 = f32[128,8]{0,1:T(8,128)} all-reduce(f32[128,8]{0,1:T(8,128)S(1)} %bitcast.54), channel_id=1, replica_groups=mesh['ep'=32,'tp'=8] {'tp'}, use_global_device_ids=true, to_apply=%region_8.9 | all-reduce | flops 1024 | bytes 8192 | tf_op jit(solution)/shard_map/psum | solution.py:82
  310.0 37.0 %all-to-all-done.3 = bf16[32,36,896]{2,1,0:T(8,128)(2,1)} async-done(((bf16[32,36,896]{2,1,0:T(8,128)(2,1)}), bf16[32,36,896]{2,1,0:T(8,128)(2,1)}, u32[]{:S(2)}, u32[]{:S(2)}) %all-to-all-start.3) | async-done | bytes 2064416 | tf_op jit(solution)/shard_map/all_to_all | solution.py:76
  347.0 2.9 fusion.12
  (2 shorter events, 0.1 us)
Async XLA Ops:
  7.2 143.6 %copy-start = (bf16[1,1024,896]{2,1,0:T(8,128)(2,1)S(1)}, bf16[1,1024,896]{2,1,0:T(8,128)(2,1)}, u32[]{:S(2)}) copy-start(bf16[1,1024,896]{2,1,0:T(8,128)(2,1)} %param.13) | copy-start | bytes 5505028
  9.0 16.0 %copy-start.2 = (pred[8,128,36]{1,2,0:T(8,128)(4,1)}, pred[8,128,36]{1,2,0:T(8,128)(4,1)S(1)}, u32[]{:S(2)}) copy-start(pred[8,128,36]{1,2,0:T(8,128)(4,1)S(1)} %iota_compare_fusion) | copy-start | bytes 110596
  9.7 15.2 %copy-start.4 = (pred[8,128,32]{1,2,0:T(8,128)(4,1)}, pred[8,128,32]{1,2,0:T(8,128)(4,1)S(1)}, u32[]{:S(2)}) copy-start(pred[8,128,32]{1,2,0:T(8,128)(4,1)S(1)} %iota_compare_fusion.2) | copy-start | bytes 98308
  13.3 11.6 %copy-start.6 = (f32[128,8]{0,1:T(8,128)S(1)}, f32[128,8]{0,1:T(8,128)}, u32[]{:S(2)}) copy-start(f32[128,8]{0,1:T(8,128)} %param.10) | copy-start | bytes 12292
  13.3 12.5 %copy-start.1 = (bf16[128,896]{1,0:T(8,128)(2,1)S(1)}, bf16[128,896]{1,0:T(8,128)(2,1)}, u32[]{:S(2)}) copy-start(bf16[128,896]{1,0:T(8,128)(2,1)} %param.8) | copy-start | bytes 688132
  13.3 65.9 %all-to-all-start = ((bf16[32,36,896]{2,1,0:T(8,128)(2,1)}), bf16[32,36,896]{2,1,0:T(8,128)(2,1)}, u32[]{:S(2)}, u32[]{:S(2)}) async-start(bf16[32,36,896]{2,1,0:T(8,128)(2,1)} %convolution_convert_fusion.3), calls=%async_computation | async-start | bytes 4587520 | tf_op jit(solution)/shard_map/all_to_all | solution.py:40
  24.9 130.2 %reduce-scatter.3.cloned.1.call-start = ((), (), s32[]{:S(2)}) async-start(), calls=%async_computation.6 | async-start | bytes 5898240 | tf_op jit(solution)/shard_map/reduce_scatter | solution.py:49
  89.0 95.6 %reduce-scatter.5.cloned.1.call-start = ((), (), s32[]{:S(2)}) async-start(), calls=%async_computation.8 | async-start | bytes 2949120 | tf_op jit(solution)/shard_map/reduce_scatter | solution.py:63
  155.1 61.2 %all-gather.3.cloned.1.call-start = ((), (), s32[]{:S(2)}) async-start(), calls=%async_computation.7 | async-start | bytes 2949120 | tf_op jit(solution)/shard_map/all_gather | solution.py:55
  157.3 99.2 %all-gather.5.cloned.1.call-start = ((), (), s32[]{:S(2)}) async-start(), calls=%async_computation.9 | async-start | bytes 5898240 | tf_op jit(solution)/shard_map/all_gather | solution.py:72
  222.4 64.6 %all-to-all-start.1 = ((bf16[32,36,896]{2,1,0:T(8,128)(2,1)}), bf16[32,36,896]{2,1,0:T(8,128)(2,1)}, u32[]{:S(2)}, u32[]{:S(2)}) async-start(bf16[32,36,896]{2,1,0:T(8,128)(2,1)} %convolution_convert_fusion.2), calls=%async_computation.2 | async-start | bytes 4587520 | tf_op jit(solution)/shard_map/all_to_all | solution.py:59
  266.2 26.4 %copy-start.3 = (pred[8,128,36]{1,2,0:T(8,128)(4,1)S(1)}, pred[8,128,36]{1,2,0:T(8,128)(4,1)}, u32[]{:S(2)}) copy-start(pred[8,128,36]{1,2,0:T(8,128)(4,1)} %copy-done.2) | copy-start | bytes 110596
  266.2 26.4 %copy-start.5 = (pred[8,128,32]{1,2,0:T(8,128)(4,1)S(1)}, pred[8,128,32]{1,2,0:T(8,128)(4,1)}, u32[]{:S(2)}) copy-start(pred[8,128,32]{1,2,0:T(8,128)(4,1)} %copy-done.4) | copy-start | bytes 98308
  287.0 60.0 %all-to-all-start.3 = ((bf16[32,36,896]{2,1,0:T(8,128)(2,1)}), bf16[32,36,896]{2,1,0:T(8,128)(2,1)}, u32[]{:S(2)}, u32[]{:S(2)}) async-start(bf16[32,36,896]{2,1,0:T(8,128)(2,1)} %fusion.9), calls=%async_computation.5 | async-start | bytes 4587520 | tf_op jit(solution)/shard_map/all_to_all | solution.py:76
Sparse Core Ops, SparseCore 0:
  89.1 36.2 reduce-scatter.2
  155.2 29.2 reduce-scatter.4
  186.4 29.8 all-gather.2
  218.0 38.4 all-gather.4

commit v4 on v3

--- a/solution.py
+++ b/solution.py
@@ -69,9 +69,11 @@
     sigma = jax.nn.sigmoid(gate_in)
     d_gate_in = (d_hidden * up_in * sigma * (1.0 + gate_in * (1.0 - sigma))).astype(jnp.bfloat16)
     d_up_in = (d_hidden * gate_in * sigma).astype(jnp.bfloat16)
-    piece = lax.all_gather(jnp.concatenate([d_gate_in, d_up_in], axis=2), "tp", axis=0, tiled=True)
-    slot_grads = jnp.einsum(
-        "gcf,df->gcd", piece, w_both, preferred_element_type=jnp.float32
+    gate_all = lax.all_gather(d_gate_in, "tp", axis=0, tiled=True)
+    up_all = lax.all_gather(d_up_in, "tp", axis=0, tiled=True)
+    slot_grads = (
+        jnp.einsum("gcf,df->gcd", gate_all, w_gate[0], preferred_element_type=jnp.float32)
+        + jnp.einsum("gcf,df->gcd", up_all, w_up[0], preferred_element_type=jnp.float32)
     ).astype(jnp.bfloat16)
     returned_grad = lax.all_to_all(slot_grads, "ep", 0, 0, tiled=True)
 

time: 358 us -> 362 us (1.011)
  waiting for transfers between devices: 190 us -> 184 us
  matrix products: 44 us -> 49.6 us
    all_to_all x1, waiting for transfers between devices: 20.8 us -> 1.05 us  [body(): returned = lax.all_to_all(outputs, 'ep', 0, 0, tiled=True)]
    all_gather x1 -> x2, waiting for transfers between devices: 24 us -> 38.1 us  [the longest x1 23.5 us: body(): up_all = lax.all_gather(d_up_in, 'tp', axis=0, tiled=True)]
    dot_general x1 -> x2, matrix products: 9.71 us -> 15.3 us  [the longest x1 8.05 us: body(): jnp.einsum('gcf,df->gcd', up_all, w_up[0], preferred_element_type=jnp.flo...]
  transfers between devices with their start and end apart: 7 -> 8, of which waited for: 6 -> 7; matrix products, arithmetic and copies ran while one was open for 9% -> 11% of each run, Pallas kernels for 0% -> 0%
where the time goes in v4:
time: 362 us; the launch traced here: 360 us
  waiting for transfers between devices  184 us (51%)
  blocking collectives  73.6 us (20%)
  matrix products  49.6 us (14%)
  starting transfers between devices  30.9 us (9%)
  between operations  13.9 us (4%)
  other arithmetic  8.12 us (2%)
    all_to_all x1, blocking collectives, body(): arrived_grad = lax.all_to_all(send_scaled, 'ep', 0, 0, tiled=True)  61.7 us
    all_to_all x1, waiting for transfers between devices, body(): arrived = lax.all_to_all(send_tokens, 'ep', 0, 0, tiled=True)  51.2 us
    all_to_all x1, waiting for transfers between devices, body(): returned_grad = lax.all_to_all(slot_grads, 'ep', 0, 0, tiled=True)  37 us
    all_gather x1, waiting for transfers between devices, body(): hidden_all = lax.all_gather(hidden, 'tp', axis=0, tiled=True)  28.9 us
    reduce_scatter x1, waiting for transfers between devices, body(): lax.psum_scatter(d_hidden_part, 'tp', scatter_dimension=0, tiled=True)  27.2 us
    all_gather x1, waiting for transfers between devices, body(): up_all = lax.all_gather(d_up_in, 'tp', axis=0, tiled=True)  23.5 us
    all_gather x1, waiting for transfers between devices, body(): gate_all = lax.all_gather(d_gate_in, 'tp', axis=0, tiled=True)  14.6 us
    psum x1, blocking collectives, body(): d_gates = lax.psum(partial_scores, 'tp')  11.9 us
  transfers between devices with their start and end apart: 8, of which 7 were waited for; matrix products, arithmetic and copies ran while one was open for 11% of the time, Pallas kernels for 0%

profile of v4, /device:TPU:24, one launch (start us, length us, event | category | flops | bytes accessed | tf_op | source)
XLA Modules:
  0.0 360.2 jit_solution(3406241422762211407)
XLA Ops:
  7.2 0.0 copy-start
  7.2 0.8 convert_reduce_fusion
  8.0 0.2 convolution_convert_fusion.4
  8.2 0.8 fusion.20
  9.0 0.0 copy-start.2
  9.0 0.7 iota_compare_fusion.2
  9.7 0.0 copy-start.4
  9.7 0.5 and_reduce_fusion
  10.3 3.1 convolution_convert_fusion.3
  13.3 0.0 copy-start.6
  13.3 0.0 copy-start.1
  13.3 11.6 %all-to-all-start = ((bf16[32,36,896]{2,1,0:T(8,128)(2,1)}), bf16[32,36,896]{2,1,0:T(8,128)(2,1)}, u32[]{:S(2)}, u32[]{:S(2)}) async-start(bf16[32,36,896]{2,1,0:T(8,128)(2,1)} %convolution_convert_fusion.3), calls=%async_computation | async-start | bytes 4587520 | tf_op jit(solution)/shard_map/all_to_all | solution.py:40
  24.9 0.0 reduce-scatter.3.cloned.1.call-start
  25.0 0.0 copy-done.2
  25.0 0.0 copy-done.4
  25.0 0.0 copy-done.6
  25.0 0.9 fusion.2
  25.8 0.0 copy-done.1
  25.8 2.2 multiply_convert_fusion
  28.0 51.2 %all-to-all-done = bf16[32,36,896]{2,1,0:T(8,128)(2,1)} async-done(((bf16[32,36,896]{2,1,0:T(8,128)(2,1)}), bf16[32,36,896]{2,1,0:T(8,128)(2,1)}, u32[]{:S(2)}, u32[]{:S(2)}) %all-to-all-start) | async-done | bytes 2064416 | tf_op jit(solution)/shard_map/all_to_all | solution.py:40
  79.2 9.7 %convolution_convert_fusion = bf16[32,36,2048]{2,1,0:T(8,128)(2,1)} fusion(bf16[32,36,896]{2,1,0:T(8,128)(2,1)} %all-to-all-done, bf16[896,1024]{1,0:T(8,128)(2,1)} %bitcast.60, bf16[896,1024]{1,0:T(8,128)(2,1)} %bitcast.59), kind=kOutput, calls=%fused_computation.7 | convolution fusion | flops 4237557760 | bytes 10452992 | tf_op jit(solution)/shard_map/gcd,df->gcf/dot_general | solution.py:44
  88.9 0.0 reduce-scatter.3.cloned.1.call-update
  89.0 0.0 reduce-scatter.5.cloned.1.call-start
  89.0 61.7 %all_to_all.20 = bf16[32,36,896]{2,1,0:T(8,128)(2,1)S(1)} all-to-all(bf16[32,36,896]{2,1,0:T(8,128)(2,1)} %multiply_convert_fusion), channel_id=1, replica_groups=mesh['ep'=32,'tp'=8] {'ep'}, dimensions={0} | all-to-all | bytes 4128768 | tf_op jit(solution)/shard_map/all_to_all | solution.py:48
  150.7 0.0 copy-done
  150.7 4.3 %convolution_convert_fusion.1 = bf16[32,36,1024]{2,1,0:T(8,128)(2,1)} fusion(bf16[32,36,896]{2,1,0:T(8,128)(2,1)S(1)} %all_to_all.20, bf16[1,1024,896]{2,1,0:T(8,128)(2,1)S(1)} %copy-done), kind=kOutput, calls=%fused_computation.18 | convolution fusion | flops 2115108864 | bytes 6258688 | tf_op jit(solution)/shard_map/gcd,fd->gcf/dot_general | solution.py:60
  155.0 0.0 reduce-scatter.5.cloned.1.call-update
  155.1 0.0 all-gather.4.cloned.1.call-start
  155.1 0.0 reduce-scatter.3.cloned.1.call-done
  155.1 1.2 convert_element_type.61
  156.4 0.9 fusion.16
  157.3 0.0 all-gather.4.cloned.1.call-update
  157.3 0.0 all-gather.6.cloned.1.call-start
  157.3 27.2 %reduce-scatter.5.cloned.1.call-done = bf16[4,36,1024]{2,1,0:T(8,128)(2,1)} async-done(((bf16[32,36,1024]{2,1,0:T(8,128)(2,1)}), bf16[4,36,1024]{2,1,0:T(8,128)(2,1)}) %reduce-scatter.5.cloned.1.call-update) | async-done | bytes 294928 | tf_op jit(solution)/shard_map/reduce_scatter | solution.py:63
  184.6 1.0 convert_element_type.66
  185.6 1.2 multiply_convert_fusion.1
  186.8 0.0 all-gather.6.cloned.1.call-update
  186.8 0.0 all-gather.8.cloned.1.call-start
  186.9 0.5 all-gather.8.cloned.1.call-update
  187.4 28.9 %all-gather.4.cloned.1.call-done = bf16[32,36,1024]{2,1,0:T(8,128)(2,1)} async-done(((bf16[4,36,1024]{2,1,0:T(8,128)(2,1)}), bf16[32,36,1024]{2,1,0:T(8,128)(2,1)}) %all-gather.4.cloned.1.call-update) | async-done | bytes 2359312 | tf_op jit(solution)/shard_map/all_gather | solution.py:55
  216.3 6.1 %convolution_convert_fusion.2 = bf16[32,36,896]{2,1,0:T(8,128)(2,1)} fusion(bf16[32,36,1024]{2,1,0:T(8,128)(2,1)} %all-gather.4.cloned.1.call-done, bf16[1,1024,896]{2,1,0:T(8,128)(2,1)S(1)} %copy-done), kind=kOutput, calls=%fused_computation.19 | convolution fusion | flops 2114961408 | bytes 6258688 | tf_op jit(solution)/shard_map/gcf,fd->gcd/dot_general | solution.py:56
  222.4 10.1 %all-to-all-start.1 = ((bf16[32,36,896]{2,1,0:T(8,128)(2,1)}), bf16[32,36,896]{2,1,0:T(8,128)(2,1)}, u32[]{:S(2)}, u32[]{:S(2)}) async-start(bf16[32,36,896]{2,1,0:T(8,128)(2,1)} %convolution_convert_fusion.2), calls=%async_computation.2 | async-start | bytes 4587520 | tf_op jit(solution)/shard_map/all_to_all | solution.py:59
  232.5 14.6 %all-gather.6.cloned.1.call-done = bf16[32,36,1024]{2,1,0:T(8,128)(2,1)} async-done(((bf16[4,36,1024]{2,1,0:T(8,128)(2,1)}), bf16[32,36,1024]{2,1,0:T(8,128)(2,1)}) %all-gather.6.cloned.1.call-update) | async-done | bytes 2359312 | tf_op jit(solution)/shard_map/all_gather | solution.py:72
  247.1 7.3 %fusion.11 = f32[32,36,896]{2,1,0:T(8,128)} fusion(bf16[32,36,1024]{2,1,0:T(8,128)(2,1)} %all-gather.6.cloned.1.call-done, bf16[1,896,1024]{2,1,0:T(8,128)(2,1)} %param.11), kind=kOutput, calls=%fused_computation.22 | convolution fusion | flops 2113929216 | bytes 8323072 | tf_op jit(solution)/shard_map/gcf,df->gcd/dot_general | solution.py:75
  254.4 23.5 %all-gather.8.cloned.1.call-done = bf16[32,36,1024]{2,1,0:T(8,128)(2,1)} async-done(((bf16[4,36,1024]{2,1,0:T(8,128)(2,1)}), bf16[32,36,1024]{2,1,0:T(8,128)(2,1)}) %all-gather.8.cloned.1.call-update) | async-done | bytes 2359312 | tf_op jit(solution)/shard_map/all_gather | solution.py:73
  277.9 8.0 %add_convert_fusion = bf16[32,36,896]{2,1,0:T(8,128)(2,1)} fusion(f32[32,36,896]{2,1,0:T(8,128)} %fusion.11, bf16[32,36,1024]{2,1,0:T(8,128)(2,1)} %all-gather.8.cloned.1.call-done, bf16[1,896,1024]{2,1,0:T(8,128)(2,1)} %param.12), kind=kOutput, calls=%fused_computation.5 | convolution fusion | flops 2115993600 | bytes 10387456 | tf_op jit(solution)/shard_map/gcf,df->gcd/dot_general | solution.py:76
  286.0 0.0 copy-start.3
  286.0 0.0 copy-start.5
  286.0 1.0 all-to-all-done.1
  287.0 9.0 %all-to-all-start.3 = ((bf16[32,36,896]{2,1,0:T(8,128)(2,1)}), bf16[32,36,896]{2,1,0:T(8,128)(2,1)}, u32[]{:S(2)}, u32[]{:S(2)}) async-start(bf16[32,36,896]{2,1,0:T(8,128)(2,1)} %add_convert_fusion), calls=%async_computation.5 | async-start | bytes 4587520 | tf_op jit(solution)/shard_map/all_to_all | solution.py:78
  296.1 0.0 copy-done.3
  296.1 0.0 copy-done.5
  296.1 5.8 %fusion.6 = (f32[8,128]{1,0:T(8,128)S(1)}, bf16[128,896]{1,0:T(8,128)(2,1)}) fusion(f32[128,896]{1,0:T(8,128)S(1)} %convert_element_type.71, f32[8,128]{1,0:T(8,128)S(1)} %bitcast.57, bf16[32,36,896]{2,1,0:T(8,128)(2,1)} %all-to-all-done.1, pred[8,128,36]{1,2,0:T(8,128)(4,1)S(1)} %copy-done.3, pred[8,128,32]{1,2,0:T(8,128)(4,1)S(1)} %copy-done.5), kind=kOutput, calls=%fused_computation.14 | convolution fusion | flops 2118663168 | bytes 2830336 | tf_op jit(solution)/shard_map/ktgc,gcd->ktd/dot_general | solution.py:81
  301.9 11.9 %psum.7 = f32[128,8]{0,1:T(8,128)} all-reduce(f32[128,8]{0,1:T(8,128)S(1)} %bitcast.58), channel_id=1, replica_groups=mesh['ep'=32,'tp'=8] {'tp'}, use_global_device_ids=true, to_apply=%region_8.9 | all-reduce | flops 1024 | bytes 8192 | tf_op jit(solution)/shard_map/psum | solution.py:84
  313.8 37.0 %all-to-all-done.3 = bf16[32,36,896]{2,1,0:T(8,128)(2,1)} async-done(((bf16[32,36,896]{2,1,0:T(8,128)(2,1)}), bf16[32,36,896]{2,1,0:T(8,128)(2,1)}, u32[]{:S(2)}, u32[]{:S(2)}) %all-to-all-start.3) | async-done | bytes 2064416 | tf_op jit(solution)/shard_map/all_to_all | solution.py:78
  350.8 2.9 fusion.15
  (2 shorter events, 0.1 us)
Async XLA Ops:
  7.2 143.5 %copy-start = (bf16[1,1024,896]{2,1,0:T(8,128)(2,1)S(1)}, bf16[1,1024,896]{2,1,0:T(8,128)(2,1)}, u32[]{:S(2)}) copy-start(bf16[1,1024,896]{2,1,0:T(8,128)(2,1)} %param.13) | copy-start | bytes 5505028
  9.0 16.0 %copy-start.2 = (pred[8,128,36]{1,2,0:T(8,128)(4,1)}, pred[8,128,36]{1,2,0:T(8,128)(4,1)S(1)}, u32[]{:S(2)}) copy-start(pred[8,128,36]{1,2,0:T(8,128)(4,1)S(1)} %iota_compare_fusion) | copy-start | bytes 110596
  9.7 15.2 %copy-start.4 = (pred[8,128,32]{1,2,0:T(8,128)(4,1)}, pred[8,128,32]{1,2,0:T(8,128)(4,1)S(1)}, u32[]{:S(2)}) copy-start(pred[8,128,32]{1,2,0:T(8,128)(4,1)S(1)} %iota_compare_fusion.2) | copy-start | bytes 98308
  13.3 11.6 %copy-start.6 = (f32[128,8]{0,1:T(8,128)S(1)}, f32[128,8]{0,1:T(8,128)}, u32[]{:S(2)}) copy-start(f32[128,8]{0,1:T(8,128)} %param.10) | copy-start | bytes 12292
  13.3 12.5 %copy-start.1 = (bf16[128,896]{1,0:T(8,128)(2,1)S(1)}, bf16[128,896]{1,0:T(8,128)(2,1)}, u32[]{:S(2)}) copy-start(bf16[128,896]{1,0:T(8,128)(2,1)} %param.8) | copy-start | bytes 688132
  13.3 65.9 %all-to-all-start = ((bf16[32,36,896]{2,1,0:T(8,128)(2,1)}), bf16[32,36,896]{2,1,0:T(8,128)(2,1)}, u32[]{:S(2)}, u32[]{:S(2)}) async-start(bf16[32,36,896]{2,1,0:T(8,128)(2,1)} %convolution_convert_fusion.3), calls=%async_computation | async-start | bytes 4587520 | tf_op jit(solution)/shard_map/all_to_all | solution.py:40
  24.9 130.2 %reduce-scatter.3.cloned.1.call-start = ((), (), s32[]{:S(2)}) async-start(), calls=%async_computation.6 | async-start | bytes 5898240 | tf_op jit(solution)/shard_map/reduce_scatter | solution.py:49
  89.0 95.6 %reduce-scatter.5.cloned.1.call-start = ((), (), s32[]{:S(2)}) async-start(), calls=%async_computation.8 | async-start | bytes 2949120 | tf_op jit(solution)/shard_map/reduce_scatter | solution.py:63
  155.1 61.2 %all-gather.4.cloned.1.call-start = ((), (), s32[]{:S(2)}) async-start(), calls=%async_computation.7 | async-start | bytes 2949120 | tf_op jit(solution)/shard_map/all_gather | solution.py:55
  157.3 89.8 %all-gather.6.cloned.1.call-start = ((), (), s32[]{:S(2)}) async-start(), calls=%async_computation.9 | async-start | bytes 2949120 | tf_op jit(solution)/shard_map/all_gather | solution.py:72
  186.8 91.1 %all-gather.8.cloned.1.call-start = ((), (), s32[]{:S(2)}) async-start(), calls=%async_computation.10 | async-start | bytes 2949120 | tf_op jit(solution)/shard_map/all_gather | solution.py:73
  222.4 64.6 %all-to-all-start.1 = ((bf16[32,36,896]{2,1,0:T(8,128)(2,1)}), bf16[32,36,896]{2,1,0:T(8,128)(2,1)}, u32[]{:S(2)}, u32[]{:S(2)}) async-start(bf16[32,36,896]{2,1,0:T(8,128)(2,1)} %convolution_convert_fusion.2), calls=%async_computation.2 | async-start | bytes 4587520 | tf_op jit(solution)/shard_map/all_to_all | solution.py:59
  286.0 10.1 %copy-start.3 = (pred[8,128,36]{1,2,0:T(8,128)(4,1)S(1)}, pred[8,128,36]{1,2,0:T(8,128)(4,1)}, u32[]{:S(2)}) copy-start(pred[8,128,36]{1,2,0:T(8,128)(4,1)} %copy-done.2) | copy-start | bytes 110596
  286.0 10.1 %copy-start.5 = (pred[8,128,32]{1,2,0:T(8,128)(4,1)S(1)}, pred[8,128,32]{1,2,0:T(8,128)(4,1)}, u32[]{:S(2)}) copy-start(pred[8,128,32]{1,2,0:T(8,128)(4,1)} %copy-done.4) | copy-start | bytes 98308
  287.0 63.7 %all-to-all-start.3 = ((bf16[32,36,896]{2,1,0:T(8,128)(2,1)}), bf16[32,36,896]{2,1,0:T(8,128)(2,1)}, u32[]{:S(2)}, u32[]{:S(2)}) async-start(bf16[32,36,896]{2,1,0:T(8,128)(2,1)} %add_convert_fusion), calls=%async_computation.5 | async-start | bytes 4587520 | tf_op jit(solution)/shard_map/all_to_all | solution.py:78
Sparse Core Ops, SparseCore 0:
  89.1 36.2 reduce-scatter.2
  155.2 29.3 reduce-scatter.4
  186.4 29.8 all-gather.3
  218.0 29.0 all-gather.5
  248.8 29.0 all-gather.7

commit v5 on v3

--- a/solution.py
+++ b/solution.py
@@ -60,8 +60,10 @@
     d_hidden_part = jnp.einsum(
         "gcd,fd->gcf", arrived_grad, wd, preferred_element_type=jnp.float32
     ).astype(jnp.bfloat16)
-    d_hidden = lax.psum_scatter(d_hidden_part, "tp", scatter_dimension=0, tiled=True).astype(
-        jnp.float32
+    ranks = lax.axis_size("tp")
+    spread = lax.all_to_all(d_hidden_part, "tp", 0, 0, tiled=True)
+    d_hidden = jnp.sum(
+        spread.reshape((ranks, -1) + spread.shape[1:]).astype(jnp.float32), axis=0
     )
     d_hidden, joined = lax.optimization_barrier((d_hidden, joined))
     gate_in = joined[:, :, :units]

time: 358 us -> 328 us (0.916)
  blocking collectives: 73.3 us -> 46.6 us
  waiting for transfers between devices: 190 us -> 183 us
    reduce_scatter x1, waiting for transfers between devices: 0.02 us -> 31.1 us  [body(): lax.psum_scatter(joined_part, 'tp', scatter_dimension=0, tiled=True)]
    all_gather x1, waiting for transfers between devices: 29.3 us -> 0.02 us  [body(): hidden_all = lax.all_gather(hidden, 'tp', axis=0, tiled=True)]
    reduce_scatter x1 -> x0, waiting for transfers between devices: 27.2 us -> none  [body(): lax.psum_scatter(d_hidden_part, 'tp', scatter_dimension=0, tiled=True)]
    all_to_all x1, blocking collectives: 61.7 us -> 35.2 us  [body(): spread = lax.all_to_all(d_hidden_part, 'tp', 0, 0, tiled=True)]
    all_to_all x0 -> x1, waiting for transfers between devices: none -> 20.6 us  [body(): arrived_grad = lax.all_to_all(send_scaled, 'ep', 0, 0, tiled=True)]
    all_to_all x0 -> x1, starting transfers between devices: none -> 5.55 us  [body(): arrived_grad = lax.all_to_all(send_scaled, 'ep', 0, 0, tiled=True)]
  transfers between devices with their start and end apart: 7 -> 7, of which waited for: 6 -> 6; matrix products, arithmetic and copies ran while one was open for 9% -> 10% of each run, Pallas kernels for 0% -> 0%
where the time goes in v5:
time: 328 us; the launch traced here: 326 us
  waiting for transfers between devices  183 us (56%)
  blocking collectives  46.6 us (14%)
  matrix products  44.5 us (14%)
  starting transfers between devices  30.6 us (9%)
  between operations  13.9 us (4%)
  other arithmetic  7.73 us (2%)
    all_to_all x1, waiting for transfers between devices, body(): arrived = lax.all_to_all(send_tokens, 'ep', 0, 0, tiled=True)  51.2 us
    all_to_all x1, waiting for transfers between devices, body(): returned_grad = lax.all_to_all(slot_grads, 'ep', 0, 0, tiled=True)  35.6 us
    all_to_all x1, blocking collectives, body(): spread = lax.all_to_all(d_hidden_part, 'tp', 0, 0, tiled=True)  35.2 us
    reduce_scatter x1, waiting for transfers between devices, body(): lax.psum_scatter(joined_part, 'tp', scatter_dimension=0, tiled=True)  31.1 us
    all_gather x1, waiting for transfers between devices, body(): lax.all_gather(jnp.concatenate([d_gate_in, d_up_in], axis=2), 'tp', axis=...  22.1 us
    all_to_all x1, waiting for transfers between devices, body(): returned = lax.all_to_all(outputs, 'ep', 0, 0, tiled=True)  22 us
    all_to_all x1, waiting for transfers between devices, body(): arrived_grad = lax.all_to_all(send_scaled, 'ep', 0, 0, tiled=True)  20.6 us
    all_to_all x1, starting transfers between devices, body(): arrived = lax.all_to_all(send_tokens, 'ep', 0, 0, tiled=True)  11.6 us
  transfers between devices with their start and end apart: 7, of which 6 were waited for; matrix products, arithmetic and copies ran while one was open for 10% of the time, Pallas kernels for 0%

profile of v5, /device:TPU:24, one launch (start us, length us, event | category | flops | bytes accessed | tf_op | source)
XLA Modules:
  0.0 326.1 jit_solution(6705754631915674836)
XLA Ops:
  7.2 0.0 copy-start
  7.2 0.8 convert_reduce_fusion.1
  8.0 0.2 convolution_convert_fusion.4
  8.2 0.8 fusion.17
  9.0 0.0 copy-start.2
  9.0 0.7 iota_compare_fusion.2
  9.7 0.0 copy-start.4
  9.7 0.5 and_reduce_fusion
  10.3 3.1 convolution_convert_fusion.3
  13.4 0.0 copy-start.6
  13.4 0.0 copy-start.1
  13.4 11.6 %all-to-all-start = ((bf16[32,36,896]{2,1,0:T(8,128)(2,1)}), bf16[32,36,896]{2,1,0:T(8,128)(2,1)}, u32[]{:S(2)}, u32[]{:S(2)}) async-start(bf16[32,36,896]{2,1,0:T(8,128)(2,1)} %convolution_convert_fusion.3), calls=%async_computation | async-start | bytes 4587520 | tf_op jit(solution)/shard_map/all_to_all | solution.py:40
  24.9 0.0 reduce-scatter.2.cloned.1.call-start
  25.0 0.0 copy-done.2
  25.0 0.0 copy-done.4
  25.0 0.0 copy-done.6
  25.0 0.9 fusion.2
  25.9 0.0 copy-done.1
  25.9 2.1 multiply_convert_fusion
  28.0 51.2 %all-to-all-done = bf16[32,36,896]{2,1,0:T(8,128)(2,1)} async-done(((bf16[32,36,896]{2,1,0:T(8,128)(2,1)}), bf16[32,36,896]{2,1,0:T(8,128)(2,1)}, u32[]{:S(2)}, u32[]{:S(2)}) %all-to-all-start) | async-done | bytes 2064416 | tf_op jit(solution)/shard_map/all_to_all | solution.py:40
  79.2 9.8 %convolution_convert_fusion = bf16[32,36,2048]{2,1,0:T(8,128)(2,1)} fusion(bf16[32,36,896]{2,1,0:T(8,128)(2,1)} %all-to-all-done, bf16[896,1024]{1,0:T(8,128)(2,1)} %bitcast.58, bf16[896,1024]{1,0:T(8,128)(2,1)} %bitcast.60), kind=kOutput, calls=%fused_computation.7 | convolution fusion | flops 4237557760 | bytes 10452992 | tf_op jit(solution)/shard_map/gcd,df->gcf/dot_general | solution.py:44
  89.0 0.0 reduce-scatter.2.cloned.1.call-update
  89.0 5.6 %all-to-all-start.2 = ((bf16[32,36,896]{2,1,0:T(8,128)(2,1)}), bf16[32,36,896]{2,1,0:T(8,128)(2,1)}, u32[]{:S(2)}, u32[]{:S(2)}) async-start(bf16[32,36,896]{2,1,0:T(8,128)(2,1)} %multiply_convert_fusion), calls=%async_computation.3 | async-start | bytes 4587520 | tf_op jit(solution)/shard_map/all_to_all | solution.py:48
  94.6 0.0 all-gather.3.cloned.1.call-start
  94.6 31.1 %reduce-scatter.2.cloned.1.call-done = bf16[4,36,2048]{2,1,0:T(8,128)(2,1)} async-done(((bf16[32,36,2048]{2,1,0:T(8,128)(2,1)}), bf16[4,36,2048]{2,1,0:T(8,128)(2,1)}) %reduce-scatter.2.cloned.1.call-update) | async-done | bytes 589840 | tf_op jit(solution)/shard_map/reduce_scatter | solution.py:49
  125.8 1.2 convert_element_type.64
  127.0 0.9 fusion.13
  127.9 0.0 all-gather.3.cloned.1.call-update
  128.0 0.0 all-gather.5.cloned.1.call-start
  128.0 20.6 %all-to-all-done.2 = bf16[32,36,896]{2,1,0:T(8,128)(2,1)} async-done(((bf16[32,36,896]{2,1,0:T(8,128)(2,1)}), bf16[32,36,896]{2,1,0:T(8,128)(2,1)}, u32[]{:S(2)}, u32[]{:S(2)}) %all-to-all-start.2) | async-done | bytes 2064416 | tf_op jit(solution)/shard_map/all_to_all | solution.py:48
  148.6 0.0 copy-done
  148.6 4.9 %convolution_convert_fusion.1 = bf16[32,36,1024]{2,1,0:T(8,128)(2,1)S(1)} fusion(bf16[32,36,896]{2,1,0:T(8,128)(2,1)} %all-to-all-done.2, bf16[1,1024,896]{2,1,0:T(8,128)(2,1)S(1)} %copy-done), kind=kOutput, calls=%fused_computation.17 | convolution fusion | flops 2115108864 | bytes 6258688 | tf_op jit(solution)/shard_map/gcd,fd->gcf/dot_general | solution.py:60
  153.5 35.2 %all_to_all.25 = bf16[32,36,1024]{2,1,0:T(8,128)(2,1)S(1)} all-to-all(bf16[32,36,1024]{2,1,0:T(8,128)(2,1)S(1)} %convolution_convert_fusion.1), channel_id=1, replica_groups=mesh['ep'=32,'tp'=8] {'tp'}, dimensions={0} | all-to-all | bytes 4718592 | tf_op jit(solution)/shard_map/all_to_all | solution.py:64
  188.7 0.5 convert_reduce_fusion
  189.2 0.4 multiply_convert_fusion.2
  189.6 0.9 pad_maximum_fusion
  190.6 0.0 all-gather.5.cloned.1.call-update
  190.6 0.0 all-gather.3.cloned.1.call-done
  190.6 6.1 %convolution_convert_fusion.2 = bf16[32,36,896]{2,1,0:T(8,128)(2,1)} fusion(bf16[32,36,1024]{2,1,0:T(8,128)(2,1)} %all-gather.3.cloned.1.call-done, bf16[1,1024,896]{2,1,0:T(8,128)(2,1)S(1)} %copy-done), kind=kOutput, calls=%fused_computation.19 | convolution fusion | flops 2114961408 | bytes 6258688 | tf_op jit(solution)/shard_map/gcf,fd->gcd/dot_general | solution.py:56
  196.7 7.2 %all-to-all-start.1 = ((bf16[32,36,896]{2,1,0:T(8,128)(2,1)}), bf16[32,36,896]{2,1,0:T(8,128)(2,1)}, u32[]{:S(2)}, u32[]{:S(2)}) async-start(bf16[32,36,896]{2,1,0:T(8,128)(2,1)} %convolution_convert_fusion.2), calls=%async_computation.2 | async-start | bytes 4587520 | tf_op jit(solution)/shard_map/all_to_all | solution.py:59
  203.9 22.1 %all-gather.5.cloned.1.call-done = bf16[32,36,2048]{2,1,0:T(8,128)(2,1)} async-done(((bf16[4,36,2048]{2,1,0:T(8,128)(2,1)}), bf16[32,36,2048]{2,1,0:T(8,128)(2,1)}) %all-gather.5.cloned.1.call-update) | async-done | bytes 4718608 | tf_op jit(solution)/shard_map/all_gather | solution.py:74
  226.0 9.7 %fusion.9 = bf16[32,36,896]{2,1,0:T(8,128)(2,1)} fusion(bf16[32,36,2048]{2,1,0:T(8,128)(2,1)} %all-gather.5.cloned.1.call-done, bf16[896,1024]{1,0:T(8,128)(2,1)} %bitcast.59, bf16[896,1024]{1,0:T(8,128)(2,1)} %bitcast.61), kind=kOutput, calls=%fused_computation.18 | convolution fusion | flops 4236230656 | bytes 10452992 | tf_op jit(solution)/shard_map/gcf,df->gcd/dot_general | solution.py:75
  235.7 0.0 copy-start.3
  235.7 0.0 copy-start.5
  235.7 22.0 %all-to-all-done.1 = bf16[32,36,896]{2,1,0:T(8,128)(2,1)} async-done(((bf16[32,36,896]{2,1,0:T(8,128)(2,1)}), bf16[32,36,896]{2,1,0:T(8,128)(2,1)}, u32[]{:S(2)}, u32[]{:S(2)}) %all-to-all-start.1) | async-done | bytes 2064416 | tf_op jit(solution)/shard_map/all_to_all | solution.py:59
  257.7 6.1 %all-to-all-start.4 = ((bf16[32,36,896]{2,1,0:T(8,128)(2,1)}), bf16[32,36,896]{2,1,0:T(8,128)(2,1)}, u32[]{:S(2)}, u32[]{:S(2)}) async-start(bf16[32,36,896]{2,1,0:T(8,128)(2,1)} %fusion.9), calls=%async_computation.5 | async-start | bytes 4587520 | tf_op jit(solution)/shard_map/all_to_all | solution.py:78
  263.8 0.0 copy-done.3
  263.9 0.0 copy-done.5
  263.9 5.8 %fusion.4 = (f32[8,128]{1,0:T(8,128)S(1)}, bf16[128,896]{1,0:T(8,128)(2,1)}) fusion(f32[128,896]{1,0:T(8,128)S(1)} %convert_element_type.75, f32[8,128]{1,0:T(8,128)S(1)} %bitcast.56, bf16[32,36,896]{2,1,0:T(8,128)(2,1)} %all-to-all-done.1, pred[8,128,36]{1,2,0:T(8,128)(4,1)S(1)} %copy-done.3, pred[8,128,32]{1,2,0:T(8,128)(4,1)S(1)} %copy-done.5), kind=kOutput, calls=%fused_computation.12 | convolution fusion | flops 2118663168 | bytes 2830336 | tf_op jit(solution)/shard_map/ktgc,gcd->ktd/dot_general | solution.py:81
  269.7 11.4 %psum.7 = f32[128,8]{0,1:T(8,128)} all-reduce(f32[128,8]{0,1:T(8,128)S(1)} %bitcast.57), channel_id=1, replica_groups=mesh['ep'=32,'tp'=8] {'tp'}, use_global_device_ids=true, to_apply=%region_8.9 | all-reduce | flops 1024 | bytes 8192 | tf_op jit(solution)/shard_map/psum | solution.py:84
  281.0 35.6 %all-to-all-done.4 = bf16[32,36,896]{2,1,0:T(8,128)(2,1)} async-done(((bf16[32,36,896]{2,1,0:T(8,128)(2,1)}), bf16[32,36,896]{2,1,0:T(8,128)(2,1)}, u32[]{:S(2)}, u32[]{:S(2)}) %all-to-all-start.4) | async-done | bytes 2064416 | tf_op jit(solution)/shard_map/all_to_all | solution.py:78
  316.6 2.9 fusion.12
  (2 shorter events, 0.1 us)
Async XLA Ops:
  7.2 141.4 %copy-start = (bf16[1,1024,896]{2,1,0:T(8,128)(2,1)S(1)}, bf16[1,1024,896]{2,1,0:T(8,128)(2,1)}, u32[]{:S(2)}) copy-start(bf16[1,1024,896]{2,1,0:T(8,128)(2,1)} %param.13) | copy-start | bytes 5505028
  9.0 16.0 %copy-start.2 = (pred[8,128,36]{1,2,0:T(8,128)(4,1)}, pred[8,128,36]{1,2,0:T(8,128)(4,1)S(1)}, u32[]{:S(2)}) copy-start(pred[8,128,36]{1,2,0:T(8,128)(4,1)S(1)} %iota_compare_fusion) | copy-start | bytes 110596
  9.7 15.3 %copy-start.4 = (pred[8,128,32]{1,2,0:T(8,128)(4,1)}, pred[8,128,32]{1,2,0:T(8,128)(4,1)S(1)}, u32[]{:S(2)}) copy-start(pred[8,128,32]{1,2,0:T(8,128)(4,1)S(1)} %iota_compare_fusion.2) | copy-start | bytes 98308
  13.4 11.6 %copy-start.6 = (f32[128,8]{0,1:T(8,128)S(1)}, f32[128,8]{0,1:T(8,128)}, u32[]{:S(2)}) copy-start(f32[128,8]{0,1:T(8,128)} %param.10) | copy-start | bytes 12292
  13.4 12.5 %copy-start.1 = (bf16[128,896]{1,0:T(8,128)(2,1)S(1)}, bf16[128,896]{1,0:T(8,128)(2,1)}, u32[]{:S(2)}) copy-start(bf16[128,896]{1,0:T(8,128)(2,1)} %param.8) | copy-start | bytes 688132
  13.4 65.9 %all-to-all-start = ((bf16[32,36,896]{2,1,0:T(8,128)(2,1)}), bf16[32,36,896]{2,1,0:T(8,128)(2,1)}, u32[]{:S(2)}, u32[]{:S(2)}) async-start(bf16[32,36,896]{2,1,0:T(8,128)(2,1)} %convolution_convert_fusion.3), calls=%async_computation | async-start | bytes 4587520 | tf_op jit(solution)/shard_map/all_to_all | solution.py:40
  24.9 100.9 %reduce-scatter.2.cloned.1.call-start = ((), (), s32[]{:S(2)}) async-start(), calls=%async_computation.6 | async-start | bytes 5898240 | tf_op jit(solution)/shard_map/reduce_scatter | solution.py:49
  89.0 59.6 %all-to-all-start.2 = ((bf16[32,36,896]{2,1,0:T(8,128)(2,1)}), bf16[32,36,896]{2,1,0:T(8,128)(2,1)}, u32[]{:S(2)}, u32[]{:S(2)}) async-start(bf16[32,36,896]{2,1,0:T(8,128)(2,1)} %multiply_convert_fusion), calls=%async_computation.3 | async-start | bytes 4587520 | tf_op jit(solution)/shard_map/all_to_all | solution.py:48
  94.6 96.0 %all-gather.3.cloned.1.call-start = ((), (), s32[]{:S(2)}) async-start(), calls=%async_computation.7 | async-start | bytes 2949120 | tf_op jit(solution)/shard_map/all_gather | solution.py:55
  128.0 98.0 %all-gather.5.cloned.1.call-start = ((), (), s32[]{:S(2)}) async-start(), calls=%async_computation.8 | async-start | bytes 5898240 | tf_op jit(solution)/shard_map/all_gather | solution.py:74
  196.7 61.0 %all-to-all-start.1 = ((bf16[32,36,896]{2,1,0:T(8,128)(2,1)}), bf16[32,36,896]{2,1,0:T(8,128)(2,1)}, u32[]{:S(2)}, u32[]{:S(2)}) async-start(bf16[32,36,896]{2,1,0:T(8,128)(2,1)} %convolution_convert_fusion.2), calls=%async_computation.2 | async-start | bytes 4587520 | tf_op jit(solution)/shard_map/all_to_all | solution.py:59
  235.7 28.2 %copy-start.3 = (pred[8,128,36]{1,2,0:T(8,128)(4,1)S(1)}, pred[8,128,36]{1,2,0:T(8,128)(4,1)}, u32[]{:S(2)}) copy-start(pred[8,128,36]{1,2,0:T(8,128)(4,1)} %copy-done.2) | copy-start | bytes 110596
  235.7 28.2 %copy-start.5 = (pred[8,128,32]{1,2,0:T(8,128)(4,1)S(1)}, pred[8,128,32]{1,2,0:T(8,128)(4,1)}, u32[]{:S(2)}) copy-start(pred[8,128,32]{1,2,0:T(8,128)(4,1)} %copy-done.4) | copy-start | bytes 98308
  257.7 58.9 %all-to-all-start.4 = ((bf16[32,36,896]{2,1,0:T(8,128)(2,1)}), bf16[32,36,896]{2,1,0:T(8,128)(2,1)}, u32[]{:S(2)}, u32[]{:S(2)}) async-start(bf16[32,36,896]{2,1,0:T(8,128)(2,1)} %fusion.9), calls=%async_computation.5 | async-start | bytes 4587520 | tf_op jit(solution)/shard_map/all_to_all | solution.py:78
Sparse Core Ops, SparseCore 0:
  89.2 36.5 reduce-scatter.1
  128.1 30.7 all-gather.2
  190.7 35.2 all-gather.4

commit v6 on v3

--- a/solution.py
+++ b/solution.py
@@ -20,7 +20,10 @@
     picks = (expert_ids.T[:, :, None, None] == jnp.arange(experts, dtype=jnp.int32)[None, None, :, None]) & (
         places.T[:, :, None, None] == jnp.arange(SLOTS, dtype=jnp.int32)[None, None, None, :]
     )
-    dispatch = jnp.any(picks, axis=0).astype(jnp.bfloat16)
+    chosen = (expert_ids[None, None, :, :] == jnp.arange(experts, dtype=jnp.int32)[:, None, None, None]) & (
+        places[None, None, :, :] == jnp.arange(SLOTS, dtype=jnp.int32)[None, :, None, None]
+    )
+    dispatch = jnp.any(chosen, axis=3).astype(jnp.bfloat16)
     return (picks, dispatch)
 
 
@@ -31,9 +34,9 @@
     units = w_gate.shape[2]
     picks, dispatch = slot_tables(expert_ids, experts)
     send_tokens = jnp.einsum(
-        "tgc,td->gcd", dispatch, tokens, preferred_element_type=jnp.float32
+        "gct,td->gcd", dispatch, tokens, preferred_element_type=jnp.float32
     ).astype(jnp.bfloat16)
-    cot_rows = jnp.einsum("tgc,td->gcd", dispatch, cotangent, preferred_element_type=jnp.float32)
+    cot_rows = jnp.einsum("gct,td->gcd", dispatch, cotangent, preferred_element_type=jnp.float32)
     slot_gate = jnp.sum(jnp.where(picks, gate_values.T[:, :, None, None], 0.0), axis=(0, 1))
     send_scaled = (slot_gate[:, :, None] * cot_rows).astype(jnp.bfloat16)
 
@@ -57,9 +60,7 @@
         jnp.bfloat16
     )
     returned = lax.all_to_all(outputs, "ep", 0, 0, tiled=True)
-    d_hidden_part = jnp.einsum(
-        "gcd,fd->gcf", arrived_grad, wd, preferred_element_type=jnp.float32
-    ).astype(jnp.bfloat16)
+    d_hidden_part = jnp.einsum("gcd,fd->gcf", arrived_grad, wd, preferred_element_type=jnp.float32).astype(jnp.bfloat16)
     d_hidden = lax.psum_scatter(d_hidden_part, "tp", scatter_dimension=0, tiled=True).astype(
         jnp.float32
     )
@@ -81,7 +82,7 @@
     partial_scores = jnp.sum(cotangent[None, :, :].astype(jnp.float32) * out_slots, axis=2).T
     d_gates = lax.psum(partial_scores, "tp")
     d_tokens = jnp.einsum(
-        "tgc,gcd->td", dispatch, returned_grad, preferred_element_type=jnp.float32
+        "gct,gcd->td", dispatch, returned_grad, preferred_element_type=jnp.float32
     ).astype(jnp.bfloat16)
     return (mixed, d_tokens, d_gates)
 

time: 358 us -> 359 us (level)
  no operation moved by 1% of the time
where the time goes in v6:
time: 359 us; the launch traced here: 358 us
  waiting for transfers between devices  189 us (53%)
  blocking collectives  73.3 us (20%)
  matrix products  43.9 us (12%)
  starting transfers between devices  27.4 us (8%)
  between operations  13.9 us (4%)
  other arithmetic  9.79 us (3%)
    all_to_all x1, blocking collectives, body(): arrived_grad = lax.all_to_all(send_scaled, 'ep', 0, 0, tiled=True)  61.7 us
    all_to_all x1, waiting for transfers between devices, body(): arrived = lax.all_to_all(send_tokens, 'ep', 0, 0, tiled=True)  50.5 us
    all_to_all x1, waiting for transfers between devices, body(): returned_grad = lax.all_to_all(slot_grads, 'ep', 0, 0, tiled=True)  37 us
    all_gather x1, waiting for transfers between devices, body(): hidden_all = lax.all_gather(hidden, 'tp', axis=0, tiled=True)  29.4 us
    reduce_scatter x1, waiting for transfers between devices, body(): lax.psum_scatter(d_hidden_part, 'tp', scatter_dimension=0, tiled=True)  27 us
    all_gather x1, waiting for transfers between devices, body(): lax.all_gather(jnp.concatenate([d_gate_in, d_up_in], axis=2), 'tp', axis=...  24.2 us
    all_to_all x1, waiting for transfers between devices, body(): returned = lax.all_to_all(outputs, 'ep', 0, 0, tiled=True)  20.8 us
    psum x1, blocking collectives, body(): d_gates = lax.psum(partial_scores, 'tp')  11.6 us
  transfers between devices with their start and end apart: 7, of which 6 were waited for; matrix products, arithmetic and copies ran while one was open for 9% of the time, Pallas kernels for 0%

profile of v6, /device:TPU:24, one launch (start us, length us, event | category | flops | bytes accessed | tf_op | source)
XLA Modules:
  0.0 357.8 jit_solution(8229210630186911040)
XLA Ops:
  7.2 0.0 copy-start
  7.2 0.8 convert_reduce_fusion
  8.0 0.7 iota_compare_fusion.2
  8.7 0.2 convolution_convert_fusion.4
  8.9 0.8 fusion.17
  9.7 2.0 and_reduce_fusion
  11.7 3.1 convolution_convert_fusion.3
  14.8 0.0 copy-start.6
  14.8 0.0 copy-start.7
  14.8 0.0 copy-start.1
  14.8 11.6 %all-to-all-start = ((bf16[32,36,896]{2,1,0:T(8,128)(2,1)}), bf16[32,36,896]{2,1,0:T(8,128)(2,1)}, u32[]{:S(2)}, u32[]{:S(2)}) async-start(bf16[32,36,896]{2,1,0:T(8,128)(2,1)} %convolution_convert_fusion.3), calls=%async_computation | async-start | bytes 4587520 | tf_op jit(solution)/shard_map/all_to_all | solution.py:43
  26.4 0.0 reduce-scatter.3.cloned.1.call-start
  26.4 0.0 copy-done.6
  26.4 0.0 copy-start.4
  26.5 0.0 copy-start.2
  26.5 0.6 copy-done.4
  27.1 0.1 copy-done.2
  27.1 0.0 copy-done.7
  27.1 0.9 fusion.2
  28.0 0.0 copy-done.1
  28.0 2.2 multiply_convert_fusion
  30.2 50.5 %all-to-all-done = bf16[32,36,896]{2,1,0:T(8,128)(2,1)} async-done(((bf16[32,36,896]{2,1,0:T(8,128)(2,1)}), bf16[32,36,896]{2,1,0:T(8,128)(2,1)}, u32[]{:S(2)}, u32[]{:S(2)}) %all-to-all-start) | async-done | bytes 2064416 | tf_op jit(solution)/shard_map/all_to_all | solution.py:43
  80.7 9.7 %convolution_convert_fusion = bf16[32,36,2048]{2,1,0:T(8,128)(2,1)} fusion(bf16[32,36,896]{2,1,0:T(8,128)(2,1)} %all-to-all-done, bf16[896,1024]{1,0:T(8,128)(2,1)} %bitcast.55, bf16[896,1024]{1,0:T(8,128)(2,1)} %bitcast.57), kind=kOutput, calls=%fused_computation.6 | convolution fusion | flops 4237557760 | bytes 10452992 | tf_op jit(solution)/shard_map/gcd,df->gcf/dot_general | solution.py:47
  90.4 0.0 reduce-scatter.3.cloned.1.call-update
  90.4 0.0 reduce-scatter.5.cloned.1.call-start
  90.5 61.7 %all_to_all.20 = bf16[32,36,896]{2,1,0:T(8,128)(2,1)S(1)} all-to-all(bf16[32,36,896]{2,1,0:T(8,128)(2,1)} %multiply_convert_fusion), channel_id=1, replica_groups=mesh['ep'=32,'tp'=8] {'ep'}, dimensions={0} | all-to-all | bytes 4128768 | tf_op jit(solution)/shard_map/all_to_all | solution.py:51
  152.2 0.0 copy-done
  152.2 4.3 %convolution_convert_fusion.1 = bf16[32,36,1024]{2,1,0:T(8,128)(2,1)} fusion(bf16[32,36,896]{2,1,0:T(8,128)(2,1)S(1)} %all_to_all.20, bf16[1,1024,896]{2,1,0:T(8,128)(2,1)S(1)} %copy-done), kind=kOutput, calls=%fused_computation.16 | convolution fusion | flops 2115108864 | bytes 6258688 | tf_op jit(solution)/shard_map/gcd,fd->gcf/dot_general | solution.py:63
  156.5 0.0 reduce-scatter.5.cloned.1.call-update
  156.5 0.0 all-gather.3.cloned.1.call-start
  156.6 0.0 reduce-scatter.3.cloned.1.call-done
  156.6 1.2 convert_element_type.61
  157.8 0.9 fusion.13
  158.7 0.0 all-gather.3.cloned.1.call-update
  158.7 0.2 all-gather.5.cloned.1.call-start
  159.0 27.0 %reduce-scatter.5.cloned.1.call-done = bf16[4,36,1024]{2,1,0:T(8,128)(2,1)} async-done(((bf16[32,36,1024]{2,1,0:T(8,128)(2,1)}), bf16[4,36,1024]{2,1,0:T(8,128)(2,1)}) %reduce-scatter.5.cloned.1.call-update) | async-done | bytes 294928 | tf_op jit(solution)/shard_map/reduce_scatter | solution.py:64
  185.9 1.0 convert_element_type.66
  187.0 0.4 multiply_convert_fusion.2
  187.4 0.9 pad_maximum_fusion
  188.3 0.0 all-gather.5.cloned.1.call-update
  188.4 29.4 %all-gather.3.cloned.1.call-done = bf16[32,36,1024]{2,1,0:T(8,128)(2,1)} async-done(((bf16[4,36,1024]{2,1,0:T(8,128)(2,1)}), bf16[32,36,1024]{2,1,0:T(8,128)(2,1)}) %all-gather.3.cloned.1.call-update) | async-done | bytes 2359312 | tf_op jit(solution)/shard_map/all_gather | solution.py:58
  217.7 6.1 %convolution_convert_fusion.2 = bf16[32,36,896]{2,1,0:T(8,128)(2,1)} fusion(bf16[32,36,1024]{2,1,0:T(8,128)(2,1)} %all-gather.3.cloned.1.call-done, bf16[1,1024,896]{2,1,0:T(8,128)(2,1)S(1)} %copy-done), kind=kOutput, calls=%fused_computation.18 | convolution fusion | flops 2114961408 | bytes 6258688 | tf_op jit(solution)/shard_map/gcf,fd->gcd/dot_general | solution.py:59
  223.8 9.9 %all-to-all-start.1 = ((bf16[32,36,896]{2,1,0:T(8,128)(2,1)}), bf16[32,36,896]{2,1,0:T(8,128)(2,1)}, u32[]{:S(2)}, u32[]{:S(2)}) async-start(bf16[32,36,896]{2,1,0:T(8,128)(2,1)} %convolution_convert_fusion.2), calls=%async_computation.2 | async-start | bytes 4587520 | tf_op jit(solution)/shard_map/all_to_all | solution.py:62
  233.7 24.2 %all-gather.5.cloned.1.call-done = bf16[32,36,2048]{2,1,0:T(8,128)(2,1)} async-done(((bf16[4,36,2048]{2,1,0:T(8,128)(2,1)}), bf16[32,36,2048]{2,1,0:T(8,128)(2,1)}) %all-gather.5.cloned.1.call-update) | async-done | bytes 4718608 | tf_op jit(solution)/shard_map/all_gather | solution.py:73
  257.9 9.7 %fusion.9 = bf16[32,36,896]{2,1,0:T(8,128)(2,1)} fusion(bf16[32,36,2048]{2,1,0:T(8,128)(2,1)} %all-gather.5.cloned.1.call-done, bf16[896,1024]{1,0:T(8,128)(2,1)} %bitcast.56, bf16[896,1024]{1,0:T(8,128)(2,1)} %bitcast.58), kind=kOutput, calls=%fused_computation.17 | convolution fusion | flops 4236230656 | bytes 10452992 | tf_op jit(solution)/shard_map/gcf,df->gcd/dot_general | solution.py:74
  267.6 0.0 copy-start.3
  267.6 0.0 copy-start.5
  267.6 20.8 %all-to-all-done.1 = bf16[32,36,896]{2,1,0:T(8,128)(2,1)} async-done(((bf16[32,36,896]{2,1,0:T(8,128)(2,1)}), bf16[32,36,896]{2,1,0:T(8,128)(2,1)}, u32[]{:S(2)}, u32[]{:S(2)}) %all-to-all-start.1) | async-done | bytes 2064416 | tf_op jit(solution)/shard_map/all_to_all | solution.py:62
  288.4 5.6 %all-to-all-start.3 = ((bf16[32,36,896]{2,1,0:T(8,128)(2,1)}), bf16[32,36,896]{2,1,0:T(8,128)(2,1)}, u32[]{:S(2)}, u32[]{:S(2)}) async-start(bf16[32,36,896]{2,1,0:T(8,128)(2,1)} %fusion.9), calls=%async_computation.5 | async-start | bytes 4587520 | tf_op jit(solution)/shard_map/all_to_all | solution.py:77
  294.0 0.0 copy-done.3
  294.0 0.0 copy-done.5
  294.1 5.8 %fusion.4 = (f32[8,128]{1,0:T(8,128)S(1)}, bf16[128,896]{1,0:T(8,128)(2,1)}) fusion(f32[128,896]{1,0:T(8,128)S(1)} %convert_element_type.71, f32[8,128]{1,0:T(8,128)S(1)} %bitcast.53, bf16[32,36,896]{2,1,0:T(8,128)(2,1)} %all-to-all-done.1, pred[8,128,36]{1,2,0:T(8,128)(4,1)S(1)} %copy-done.3, pred[8,128,32]{1,2,0:T(8,128)(4,1)S(1)} %copy-done.5), kind=kOutput, calls=%fused_computation.11 | convolution fusion | flops 2118663168 | bytes 2830336 | tf_op jit(solution)/shard_map/ktgc,gcd->ktd/dot_general | solution.py:80
  299.9 11.6 %psum.7 = f32[128,8]{0,1:T(8,128)} all-reduce(f32[128,8]{0,1:T(8,128)S(1)} %bitcast.54), channel_id=1, replica_groups=mesh['ep'=32,'tp'=8] {'tp'}, use_global_device_ids=true, to_apply=%region_8.9 | all-reduce | flops 1024 | bytes 8192 | tf_op jit(solution)/shard_map/psum | solution.py:83
  311.5 37.0 %all-to-all-done.3 = bf16[32,36,896]{2,1,0:T(8,128)(2,1)} async-done(((bf16[32,36,896]{2,1,0:T(8,128)(2,1)}), bf16[32,36,896]{2,1,0:T(8,128)(2,1)}, u32[]{:S(2)}, u32[]{:S(2)}) %all-to-all-start.3) | async-done | bytes 2064416 | tf_op jit(solution)/shard_map/all_to_all | solution.py:77
  348.4 2.9 fusion.12
  (4 shorter events, 0.1 us)
Async XLA Ops:
  7.2 145.0 %copy-start = (bf16[1,1024,896]{2,1,0:T(8,128)(2,1)S(1)}, bf16[1,1024,896]{2,1,0:T(8,128)(2,1)}, u32[]{:S(2)}) copy-start(bf16[1,1024,896]{2,1,0:T(8,128)(2,1)} %param.13) | copy-start | bytes 5505028
  14.8 11.6 %copy-start.6 = (s32[128,8]{0,1:T(8,128)S(1)}, s32[128,8]{0,1:T(8,128)}, u32[]{:S(2)}) copy-start(s32[128,8]{0,1:T(8,128)} %param.9) | copy-start | bytes 12292
  14.8 12.3 %copy-start.7 = (f32[128,8]{0,1:T(8,128)S(1)}, f32[128,8]{0,1:T(8,128)}, u32[]{:S(2)}) copy-start(f32[128,8]{0,1:T(8,128)} %param.10) | copy-start | bytes 12292
  14.8 13.2 %copy-start.1 = (bf16[128,896]{1,0:T(8,128)(2,1)S(1)}, bf16[128,896]{1,0:T(8,128)(2,1)}, u32[]{:S(2)}) copy-start(bf16[128,896]{1,0:T(8,128)(2,1)} %param.8) | copy-start | bytes 688132
  14.8 65.9 %all-to-all-start = ((bf16[32,36,896]{2,1,0:T(8,128)(2,1)}), bf16[32,36,896]{2,1,0:T(8,128)(2,1)}, u32[]{:S(2)}, u32[]{:S(2)}) async-start(bf16[32,36,896]{2,1,0:T(8,128)(2,1)} %convolution_convert_fusion.3), calls=%async_computation | async-start | bytes 4587520 | tf_op jit(solution)/shard_map/all_to_all | solution.py:43
  26.4 130.2 %reduce-scatter.3.cloned.1.call-start = ((), (), s32[]{:S(2)}) async-start(), calls=%async_computation.6 | async-start | bytes 5898240 | tf_op jit(solution)/shard_map/reduce_scatter | solution.py:52
  26.4 0.6 copy-start.4
  26.5 0.6 copy-start.2
  90.4 95.5 %reduce-scatter.5.cloned.1.call-start = ((), (), s32[]{:S(2)}) async-start(), calls=%async_computation.8 | async-start | bytes 2949120 | tf_op jit(solution)/shard_map/reduce_scatter | solution.py:64
  156.5 61.2 %all-gather.3.cloned.1.call-start = ((), (), s32[]{:S(2)}) async-start(), calls=%async_computation.7 | async-start | bytes 2949120 | tf_op jit(solution)/shard_map/all_gather | solution.py:58
  158.7 99.2 %all-gather.5.cloned.1.call-start = ((), (), s32[]{:S(2)}) async-start(), calls=%async_computation.9 | async-start | bytes 5898240 | tf_op jit(solution)/shard_map/all_gather | solution.py:73
  223.8 64.6 %all-to-all-start.1 = ((bf16[32,36,896]{2,1,0:T(8,128)(2,1)}), bf16[32,36,896]{2,1,0:T(8,128)(2,1)}, u32[]{:S(2)}, u32[]{:S(2)}) async-start(bf16[32,36,896]{2,1,0:T(8,128)(2,1)} %convolution_convert_fusion.2), calls=%async_computation.2 | async-start | bytes 4587520 | tf_op jit(solution)/shard_map/all_to_all | solution.py:62
  267.6 26.4 %copy-start.3 = (pred[8,128,36]{1,2,0:T(8,128)(4,1)S(1)}, pred[8,128,36]{1,2,0:T(8,128)(4,1)}, u32[]{:S(2)}) copy-start(pred[8,128,36]{1,2,0:T(8,128)(4,1)} %copy-done.2) | copy-start | bytes 110596
  267.6 26.4 %copy-start.5 = (pred[8,128,32]{1,2,0:T(8,128)(4,1)S(1)}, pred[8,128,32]{1,2,0:T(8,128)(4,1)}, u32[]{:S(2)}) copy-start(pred[8,128,32]{1,2,0:T(8,128)(4,1)} %copy-done.4) | copy-start | bytes 98308
  288.4 60.0 %all-to-all-start.3 = ((bf16[32,36,896]{2,1,0:T(8,128)(2,1)}), bf16[32,36,896]{2,1,0:T(8,128)(2,1)}, u32[]{:S(2)}, u32[]{:S(2)}) async-start(bf16[32,36,896]{2,1,0:T(8,128)(2,1)} %fusion.9), calls=%async_computation.5 | async-start | bytes 4587520 | tf_op jit(solution)/shard_map/all_to_all | solution.py:77
Sparse Core Ops, SparseCore 0:
  90.5 36.2 reduce-scatter.2
  156.6 29.2 reduce-scatter.4
  187.8 29.8 all-gather.2
  219.4 38.4 all-gather.4
